TPU v7x, 256 devices: a whole 4x4x8 slice. The times are simulated.
256 devices in a mesh: leaf: 4 (over x), row: 4 (over y), col: 16 (over z, core).
Axes of the slice: x: 4, y: 4, z: 8, core: 2. Of those that a mesh axis runs over, the one named last changes fastest.
Arguments:
- local_inv: float32 [4, 4, 256, 128, 128], P('leaf', 'row', 'col'), may hold values from -2 to 2, as said below
- local_off: float32 [4, 4, 256, 2, 128, 128], P('leaf', 'row', 'col'), may hold values from -0.09375 to 0.09375
- local_dep: int32 [4, 4, 256, 2], P('leaf', 'row', 'col'), may hold values from 0 to 7
- local_rhs: float32 [4, 4, 256, 64, 128], P('leaf', 'row', 'col'), may hold values from -6 to 6
- top_inv: float32 [8, 4, 16, 128, 128], P(None, 'row', 'col'), may hold values from -2 to 2, as said below
- top_off: float32 [7, 4, 16, 4, 128, 128], P(None, 'row', 'col'), may hold values from -0.125 to 0.125
- top_dep: int32 [7, 4, 16, 4], P(None, 'row', 'col'), may hold values from 0 to 19
- top_rhs: float32 [8, 4, 16, 64, 128], P(None, 'row', 'col'), may hold values from -6 to 6
Outputs:
- local_sol: float32 [4, 4, 256, 64, 128], P('leaf', 'row', 'col')
- top_sol: float32 [8, 4, 16, 64, 128], P(None, 'row', 'col')
Inputs may be any that keep to these rules, and one draw needn't show every extreme that they name: `local_inv`: lower-triangular inverse diagonal blocks of a Cholesky factor: entry [t, s] is zero for s > t. `top_inv`: lower-triangular inverse diagonal blocks of a Cholesky factor: entry [t, s] is zero for s > t. `local_dep`: levels of ancestors owned by the supernode's own grid cell. `top_dep`: a value v < 16 names the supernode one level lower in cell (r, v); a value v >= 16 the one in cell (v - 16, c).
All inputs are finite; a program needn't handle non-finite values.
Results may differ from a plain program's by a relative error of at most 0.0001.
Values sent between devices are 32-bit elements; how exact they have to be, the bound alone decides.
No kernel may reach another device: no remote copies, remote signals or barrier semaphores. Data moves between devices by JAX's collectives and lax.ppermute only.
A program may use at most 64 MiB of HBM per device.

v0:
```python
import jax
import jax.numpy as jnp
from jax import lax
from jax.sharding import PartitionSpec as P

highest = lax.Precision.HIGHEST


def apply_inverse(inverse, block):
    return jnp.einsum("rs,ts->rt", block, inverse, precision=highest)


def apply_transpose(inverse, block):
    return jnp.einsum("rs,st->rt", block, inverse, precision=highest)


def shifted(value, axis, k):
    n = lax.axis_size(axis)
    return lax.ppermute(value, axis, [(i, (i + k) % n) for i in range(n)])


def select_sum(mask, stacked):
    mask = mask.reshape(mask.shape + (1,) * (stacked.ndim - 1))
    return jnp.sum(jnp.where(mask, stacked[None], 0.0), axis=1)


def spread_sum(mask, pieces):
    return jnp.sum(jnp.where(mask[:, :, None, None], pieces[:, None], 0.0), axis=0)


def gather_sources(block, col_pick, row_pick):
    by_col = lax.all_gather(block[None], "col", axis=0, tiled=True)
    n_row = lax.axis_size("row")
    by_shift = jnp.stack([block] + [shifted(block, "row", k) for k in range(1, n_row)])
    return select_sum(col_pick, by_col) + select_sum(row_pick, by_shift)


def push_back(pieces, col_pick, row_push):
    n_row = lax.axis_size("row")
    slots = spread_sum(col_pick, pieces)
    incoming = lax.all_to_all(slots, "col", 0, 0, tiled=True).sum(0)
    parts = spread_sum(row_push, pieces)
    incoming = incoming + parts[0]
    for k in range(1, n_row):
        incoming = incoming + shifted(parts[k], "row", k)
    return incoming


def solve_top(top_inverse, top_blocks, top_links, top_right, updates):
    levels = top_inverse.shape[0]
    width_cols = lax.axis_size("col")
    n_row = lax.axis_size("row")
    me_row = lax.axis_index("row")
    is_col = top_links < width_cols
    col_pick = top_links[..., None] == jnp.arange(width_cols, dtype=jnp.int32)
    pull = jnp.mod(me_row - (top_links - width_cols), n_row)
    push = jnp.mod(top_links - width_cols - me_row, n_row)
    shifts = jnp.arange(n_row, dtype=jnp.int32)
    row_pick = (~is_col)[..., None] & (pull[..., None] == shifts)
    row_push = (~is_col)[..., None] & (push[..., None] == shifts)
    forward = []
    for height in range(levels):
        target = top_right[height] - updates[height]
        if height > 0:
            picked = gather_sources(forward[-1], col_pick[height - 1], row_pick[height - 1])
            target = target - jnp.einsum(
                "jrs,jts->rt", picked, top_blocks[height - 1], precision=highest
            )
        forward.append(apply_inverse(top_inverse[height], target))
    forward = jnp.stack(forward)
    current = apply_transpose(top_inverse[levels - 1], forward[levels - 1])
    solved = jnp.zeros_like(forward).at[levels - 1].set(current)

    def step(i, carry):
        current, solved = carry
        height = levels - 2 - i
        at = lambda a: lax.dynamic_index_in_dim(a, height, 0, keepdims=False)
        pieces = jnp.einsum("rt,jts->jrs", current, at(top_blocks), precision=highest)
        incoming = push_back(pieces, at(col_pick), at(row_push))
        current = apply_transpose(at(top_inverse), at(forward) - incoming)
        return current, lax.dynamic_update_index_in_dim(solved, current, height, 0)

    return lax.fori_loop(0, levels - 1, step, (current, solved))[1]


def on_device(local_inv, local_off, local_dep, local_rhs, top_inv, top_off, top_dep, top_rhs):
    inverse = local_inv[0, 0]
    blocks = local_off[0, 0]
    ancestor_levels = local_dep[0, 0]
    right_local = local_rhs[0, 0]
    levels = top_inv.shape[0]
    top_inverse = top_inv[:, 0, 0]
    top_blocks = top_off[:, 0, 0]
    top_links = top_dep[:, 0, 0]
    top_right = top_rhs[:, 0, 0]
    local_first = jnp.einsum("krs,kts->krt", right_local, inverse, precision=highest)
    contributions = jnp.einsum("krs,kjts->kjrt", local_first, blocks, precision=highest)
    level_matches = (ancestor_levels[:, :, None] == jnp.arange(levels, dtype=jnp.int32)).astype(
        jnp.float32
    )
    updates = jnp.einsum("kjl,kjrt->lrt", level_matches, contributions, precision=highest)
    n_leaf = lax.axis_size("leaf")
    by_shift = jnp.stack([updates] + [shifted(updates, "leaf", k) for k in range(1, n_leaf)])
    order = jnp.mod(lax.axis_index("leaf") - jnp.arange(n_leaf, dtype=jnp.int32), n_leaf)
    weights = order[:, None] == jnp.arange(n_leaf, dtype=jnp.int32)
    ordered = select_sum(weights, by_shift)
    totals = ordered[0]
    for u in range(1, n_leaf):
        totals = totals + ordered[u]
    top_solution = solve_top(top_inverse, top_blocks, top_links, top_right, totals)
    ancestors = jnp.einsum("kjl,lrt->kjrt", level_matches, top_solution, precision=highest)
    remainder = local_first - jnp.einsum("kjrt,kjts->krs", ancestors, blocks, precision=highest)
    local_solution = jnp.einsum("krs,kst->krt", remainder, inverse, precision=highest)
    return (local_solution[None, None], top_solution[:, None, None])


def solution(mesh):
    placed = (
        P("leaf", "row", "col", None, None),
        P("leaf", "row", "col", None, None, None),
        P("leaf", "row", "col", None),
        P("leaf", "row", "col", None, None),
        P(None, "row", "col", None, None),
        P(None, "row", "col", None, None, None),
        P(None, "row", "col", None),
        P(None, "row", "col", None, None),
    )
    return jax.shard_map(
        on_device,
        mesh=mesh,
        in_specs=placed,
        out_specs=(P("leaf", "row", "col", None, None), P(None, "row", "col", None, None)),
        check_vma=False,
    )
```

profile of v0, /device:TPU:2, one launch (start us, length us, event | category | flops | bytes accessed | tf_op | source)
XLA Modules:
  0.0 376.3 jit_solution(4697018135431169076)
XLA Ops:
  0.6 3.7 fusion.36
  4.3 2.3 fusion.18
  7.8 1.6 collective-permute-start.3
  9.3 2.8 collective-permute-start.4
  13.3 3.9 %collective-permute-done.3 = f32[8,64,128]{2,0,1:T(8,128)S(1)} collective-permute-done((f32[8,64,128]{2,0,1:T(8,128)S(1)}, f32[8,64,128]{2,0,1:T(8,128)S(1)}, u32[]{:S(2)}, u32[]{:S(2)}) %collective-permute-start.3) | collective-permute-done | bytes 262176 | tf_op jit(solution)/shard_map/ppermute | solution.py:19
  17.2 2.8 collective-permute-done.4
  20.0 3.5 collective-permute-done.5
  26.4 1.8 collective-permute-start.6
  28.2 2.9 collective-permute-start.7
  32.4 21.4 %all-gather = f32[1024,128]{1,0:T(8,128)S(1)} all-gather(f32[64,128]{1,0:T(8,128)S(1)} %get-tuple-element.254), channel_id=2, replica_groups=mesh['leaf'=4,'row'=4,'col'=16] {'col'}, dimensions={0}, use_global_device_ids=true | all-gather | bytes 557056 | tf_op jit(solution)/shard_map/all_gather | solution.py:32
  54.2 1.4 fusion.32
  58.2 2.0 collective-permute-start.11
  60.2 15.7 %all-gather.1 = f32[1024,128]{1,0:T(8,128)S(1)} all-gather(f32[64,128]{1,0:T(8,128)S(1)} %get-tuple-element.256), channel_id=3, replica_groups=mesh['leaf'=4,'row'=4,'col'=16] {'col'}, dimensions={0}, use_global_device_ids=true | all-gather | bytes 557056 | tf_op jit(solution)/shard_map/all_gather | solution.py:32
  76.3 1.4 fusion.31
  79.5 2.2 collective-permute-start.13
  81.6 2.5 collective-permute-start.14
  84.2 17.4 %all-gather.2 = f32[1024,128]{1,0:T(8,128)S(1)} all-gather(f32[64,128]{1,0:T(8,128)S(1)} %get-tuple-element.258), channel_id=4, replica_groups=mesh['leaf'=4,'row'=4,'col'=16] {'col'}, dimensions={0}, use_global_device_ids=true | all-gather | bytes 557056 | tf_op jit(solution)/shard_map/all_gather | solution.py:32
  101.9 1.4 fusion.30
  104.5 1.5 collective-permute-start.16
  105.9 2.0 collective-permute-start.17
  107.9 15.7 %all-gather.3 = f32[1024,128]{1,0:T(8,128)S(1)} all-gather(f32[64,128]{1,0:T(8,128)S(1)} %get-tuple-element.260), channel_id=5, replica_groups=mesh['leaf'=4,'row'=4,'col'=16] {'col'}, dimensions={0}, use_global_device_ids=true | all-gather | bytes 557056 | tf_op jit(solution)/shard_map/all_gather | solution.py:32
  127.2 2.2 collective-permute-start.19
  129.4 2.5 collective-permute-start.20
  131.9 17.4 %all-gather.4 = f32[1024,128]{1,0:T(8,128)S(1)} all-gather(f32[64,128]{1,0:T(8,128)S(1)} %get-tuple-element.262), channel_id=6, replica_groups=mesh['leaf'=4,'row'=4,'col'=16] {'col'}, dimensions={0}, use_global_device_ids=true | all-gather | bytes 557056 | tf_op jit(solution)/shard_map/all_gather | solution.py:32
  152.2 1.5 collective-permute-start.22
  153.7 2.0 collective-permute-start.23
  155.6 15.9 %all-gather.5 = f32[1024,128]{1,0:T(8,128)S(1)} all-gather(f32[64,128]{1,0:T(8,128)S(1)} %get-tuple-element.264), channel_id=7, replica_groups=mesh['leaf'=4,'row'=4,'col'=16] {'col'}, dimensions={0}, use_global_device_ids=true | all-gather | bytes 557056 | tf_op jit(solution)/shard_map/all_gather | solution.py:32
  172.0 1.4 fusion.27
  175.1 2.2 collective-permute-start.25
  177.3 2.5 collective-permute-start.26
  179.8 17.4 %all-gather.6 = f32[1024,128]{1,0:T(8,128)S(1)} all-gather(f32[64,128]{1,0:T(8,128)S(1)} %get-tuple-element.266), channel_id=8, replica_groups=mesh['leaf'=4,'row'=4,'col'=16] {'col'}, dimensions={0}, use_global_device_ids=true | all-gather | bytes 557056 | tf_op jit(solution)/shard_map/all_gather | solution.py:32
  197.6 1.4 fusion.26
  201.9 168.9 %while.18 = (s32[]{:T(128)}, f32[64,128]{1,0:T(8,128)S(1)}, f32[8,64,128]{2,1,0:T(8,128)}, f32[8,64,128]{2,1,0:T(8,128)}, pred[7,4,16]{2,1,0:T(4,128)(4,1)S(1)},...) while((s32[]{:T(128)}, f32[64,128]{1,0:T(8,128)S(1)}, ...), condition=%wide.region_19.20_spmd, body=%wide.region_15.19_spmd.sunk | while | flops 64225288 | bytes 4393060 | solution.py:83
  204.2 3.7 all-to-all-start
  208.1 1.5 collective-permute-start.1
  210.4 13.5 %all-to-all-done = f32[16,64,128]{2,1,0:T(8,128)S(1)} async-done(((f32[16,64,128]{2,1,0:T(8,128)}), f32[16,64,128]{2,1,0:T(8,128)S(1)}, u32[]{:S(2)}, u32[]{:S(2)}) %all-to-all-start) | async-done | bytes 524320 | tf_op jit(solution)/shard_map/while/body/eval_jaxpr/all_to_all | solution.py:41
  223.9 1.7 bitcast_dynamic-update-slice_fusion.3
  227.8 4.2 %all-to-all-start = ((f32[16,64,128]{2,1,0:T(8,128)}), f32[16,64,128]{2,1,0:T(8,128)S(1)}, u32[]{:S(2)}, u32[]{:S(2)}) async-start(f32[16,64,128]{2,1,0:T(8,128)} %select_reduce_fusion.20), calls=%async_computation | async-start | bytes 1048576 | tf_op jit(solution)/shard_map/while/body/eval_jaxpr/all_to_all | solution.py:41
  232.3 1.5 collective-permute-start.1
  234.5 13.7 %all-to-all-done = f32[16,64,128]{2,1,0:T(8,128)S(1)} async-done(((f32[16,64,128]{2,1,0:T(8,128)}), f32[16,64,128]{2,1,0:T(8,128)S(1)}, u32[]{:S(2)}, u32[]{:S(2)}) %all-to-all-start) | async-done | bytes 524320 | tf_op jit(solution)/shard_map/while/body/eval_jaxpr/all_to_all | solution.py:41
  248.3 1.7 bitcast_dynamic-update-slice_fusion.3
  252.2 4.0 %all-to-all-start = ((f32[16,64,128]{2,1,0:T(8,128)}), f32[16,64,128]{2,1,0:T(8,128)S(1)}, u32[]{:S(2)}, u32[]{:S(2)}) async-start(f32[16,64,128]{2,1,0:T(8,128)} %select_reduce_fusion.20), calls=%async_computation | async-start | bytes 1048576 | tf_op jit(solution)/shard_map/while/body/eval_jaxpr/all_to_all | solution.py:41
  256.5 1.5 collective-permute-start.1
  258.7 13.7 %all-to-all-done = f32[16,64,128]{2,1,0:T(8,128)S(1)} async-done(((f32[16,64,128]{2,1,0:T(8,128)}), f32[16,64,128]{2,1,0:T(8,128)S(1)}, u32[]{:S(2)}, u32[]{:S(2)}) %all-to-all-start) | async-done | bytes 524320 | tf_op jit(solution)/shard_map/while/body/eval_jaxpr/all_to_all | solution.py:41
  272.5 1.7 bitcast_dynamic-update-slice_fusion.3
  276.4 4.0 %all-to-all-start = ((f32[16,64,128]{2,1,0:T(8,128)}), f32[16,64,128]{2,1,0:T(8,128)S(1)}, u32[]{:S(2)}, u32[]{:S(2)}) async-start(f32[16,64,128]{2,1,0:T(8,128)} %select_reduce_fusion.20), calls=%async_computation | async-start | bytes 1048576 | tf_op jit(solution)/shard_map/while/body/eval_jaxpr/all_to_all | solution.py:41
  280.7 1.5 collective-permute-start.1
  282.9 13.7 %all-to-all-done = f32[16,64,128]{2,1,0:T(8,128)S(1)} async-done(((f32[16,64,128]{2,1,0:T(8,128)}), f32[16,64,128]{2,1,0:T(8,128)S(1)}, u32[]{:S(2)}, u32[]{:S(2)}) %all-to-all-start) | async-done | bytes 524320 | tf_op jit(solution)/shard_map/while/body/eval_jaxpr/all_to_all | solution.py:41
  296.6 1.7 bitcast_dynamic-update-slice_fusion.3
  300.5 4.0 %all-to-all-start = ((f32[16,64,128]{2,1,0:T(8,128)}), f32[16,64,128]{2,1,0:T(8,128)S(1)}, u32[]{:S(2)}, u32[]{:S(2)}) async-start(f32[16,64,128]{2,1,0:T(8,128)} %select_reduce_fusion.20), calls=%async_computation | async-start | bytes 1048576 | tf_op jit(solution)/shard_map/while/body/eval_jaxpr/all_to_all | solution.py:41
  304.8 1.5 collective-permute-start.1
  307.0 13.7 %all-to-all-done = f32[16,64,128]{2,1,0:T(8,128)S(1)} async-done(((f32[16,64,128]{2,1,0:T(8,128)}), f32[16,64,128]{2,1,0:T(8,128)S(1)}, u32[]{:S(2)}, u32[]{:S(2)}) %all-to-all-start) | async-done | bytes 524320 | tf_op jit(solution)/shard_map/while/body/eval_jaxpr/all_to_all | solution.py:41
  320.8 1.7 bitcast_dynamic-update-slice_fusion.3
  324.7 4.0 %all-to-all-start = ((f32[16,64,128]{2,1,0:T(8,128)}), f32[16,64,128]{2,1,0:T(8,128)S(1)}, u32[]{:S(2)}, u32[]{:S(2)}) async-start(f32[16,64,128]{2,1,0:T(8,128)} %select_reduce_fusion.20), calls=%async_computation | async-start | bytes 1048576 | tf_op jit(solution)/shard_map/while/body/eval_jaxpr/all_to_all | solution.py:41
  329.0 1.5 collective-permute-start.1
  331.2 13.7 %all-to-all-done = f32[16,64,128]{2,1,0:T(8,128)S(1)} async-done(((f32[16,64,128]{2,1,0:T(8,128)}), f32[16,64,128]{2,1,0:T(8,128)S(1)}, u32[]{:S(2)}, u32[]{:S(2)}) %all-to-all-start) | async-done | bytes 524320 | tf_op jit(solution)/shard_map/while/body/eval_jaxpr/all_to_all | solution.py:41
  345.0 1.7 bitcast_dynamic-update-slice_fusion.3
  348.9 4.0 %all-to-all-start = ((f32[16,64,128]{2,1,0:T(8,128)}), f32[16,64,128]{2,1,0:T(8,128)S(1)}, u32[]{:S(2)}, u32[]{:S(2)}) async-start(f32[16,64,128]{2,1,0:T(8,128)} %select_reduce_fusion.20), calls=%async_computation | async-start | bytes 1048576 | tf_op jit(solution)/shard_map/while/body/eval_jaxpr/all_to_all | solution.py:41
  353.2 1.5 collective-permute-start.1
  355.4 13.7 %all-to-all-done = f32[16,64,128]{2,1,0:T(8,128)S(1)} async-done(((f32[16,64,128]{2,1,0:T(8,128)}), f32[16,64,128]{2,1,0:T(8,128)S(1)}, u32[]{:S(2)}, u32[]{:S(2)}) %all-to-all-start) | async-done | bytes 524320 | tf_op jit(solution)/shard_map/while/body/eval_jaxpr/all_to_all | solution.py:41
  369.1 1.7 bitcast_dynamic-update-slice_fusion.3
  370.8 1.6 fusion.49
  372.4 1.9 fusion.23
  374.4 1.9 convolution_bitcast_fusion.1
  (176 shorter events, 46.8 us)
Async XLA Ops:
  0.6 3.7 copy-start
  4.3 2.4 copy-start.5
  4.3 8.3 %copy-start.4 = (s32[7,1,1,4]{0,3,2,1:T(4,128)S(1)}, s32[7,1,1,4]{0,3,2,1:T(4,128)}, u32[]{:S(2)}) copy-start(s32[7,1,1,4]{0,3,2,1:T(4,128)} %param.18) | copy-start | bytes 340
  7.8 9.5 %collective-permute-start.3 = (f32[8,64,128]{2,0,1:T(8,128)S(1)}, f32[8,64,128]{2,0,1:T(8,128)S(1)}, u32[]{:S(2)}, u32[]{:S(2)}) collective-permute-start(f32[8,64,128]{2,0,1:T(8,128)S(1)} %bitcast.376), channel_id=1, source_target_pairs={{0,64},{64,128},{128,192},{192,0},{1,65},{65,129},{129,193},{193,1... | collective-permute-start | bytes 786440 | tf_op jit(solution)/shard_map/ppermute | solution.py:19
  9.3 10.7 %collective-permute-start.4 = (f32[8,64,128]{2,0,1:T(8,128)S(1)}, f32[8,64,128]{2,0,1:T(8,128)S(1)}, u32[]{:S(2)}, u32[]{:S(2)}) collective-permute-start(f32[8,64,128]{2,0,1:T(8,128)S(1)} %bitcast.377), channel_id=1, source_target_pairs={{0,128},{64,192},{128,0},{192,64},{1,129},{65,193},{129,1},{193,65... | collective-permute-start | bytes 786440 | tf_op jit(solution)/shard_map/ppermute | solution.py:19
  12.1 11.4 %collective-permute-start.5 = (f32[8,64,128]{2,0,1:T(8,128)S(1)}, f32[8,64,128]{2,0,1:T(8,128)}, u32[]{:S(2)}, u32[]{:S(2)}) collective-permute-start(f32[8,64,128]{2,0,1:T(8,128)S(1)} %bitcast.378), channel_id=1, source_target_pairs={{0,192},{64,0},{128,64},{192,128},{1,193},{65,1},{129,65},{193,129... | collective-permute-start | bytes 786440 | tf_op jit(solution)/shard_map/ppermute | solution.py:19
  25.2 29.0 %copy-start.2 = (f32[1,8,64,128]{3,2,1,0:T(8,128)}, f32[1,8,64,128]{3,2,1,0:T(8,128)S(1)}, u32[]{:S(2)}) copy-start(f32[1,8,64,128]{3,2,1,0:T(8,128)S(1)} %slice_add_fusion) | copy-start | bytes 786436
  26.4 27.6 %collective-permute-start.6 = (f32[64,128]{1,0:T(8,128)S(1)}, f32[64,128]{1,0:T(8,128)S(1)}, u32[]{:S(2)}, u32[]{:S(2)}) collective-permute-start(f32[64,128]{1,0:T(8,128)S(1)} %get-tuple-element.254), channel_id=1, source_target_pairs={{0,16},{16,32},{32,48},{48,0},{1,17},{17,33},{33,49},{49,1},{2,18}... | collective-permute-start | bytes 98312 | tf_op jit(solution)/shard_map/ppermute | solution.py:19
  28.2 25.9 %collective-permute-start.7 = (f32[64,128]{1,0:T(8,128)S(1)}, f32[64,128]{1,0:T(8,128)S(1)}, u32[]{:S(2)}, u32[]{:S(2)}) collective-permute-start(f32[64,128]{1,0:T(8,128)S(1)} %get-tuple-element.254), channel_id=1, source_target_pairs={{0,32},{16,48},{32,0},{48,16},{1,33},{17,49},{33,1},{49,17},{2,34}... | collective-permute-start | bytes 98312 | tf_op jit(solution)/shard_map/ppermute | solution.py:19
  31.1 23.0 %collective-permute-start.8 = (f32[64,128]{1,0:T(8,128)S(1)}, f32[64,128]{1,0:T(8,128)S(1)}, u32[]{:S(2)}, u32[]{:S(2)}) collective-permute-start(f32[64,128]{1,0:T(8,128)S(1)} %get-tuple-element.254), channel_id=1, source_target_pairs={{0,48},{16,0},{32,16},{48,32},{1,49},{17,1},{33,17},{49,33},{2,50}... | collective-permute-start | bytes 98312 | tf_op jit(solution)/shard_map/ppermute | solution.py:19
  56.7 19.5 %collective-permute-start.9 = (f32[64,128]{1,0:T(8,128)S(1)}, f32[64,128]{1,0:T(8,128)S(1)}, u32[]{:S(2)}, u32[]{:S(2)}) collective-permute-start(f32[64,128]{1,0:T(8,128)S(1)} %get-tuple-element.256), channel_id=1, source_target_pairs={{0,16},{16,32},{32,48},{48,0},{1,17},{17,33},{33,49},{49,1},{2,18}... | collective-permute-start | bytes 98312 | tf_op jit(solution)/shard_map/ppermute | solution.py:19
  57.4 18.7 %collective-permute-start.10 = (f32[64,128]{1,0:T(8,128)S(1)}, f32[64,128]{1,0:T(8,128)S(1)}, u32[]{:S(2)}, u32[]{:S(2)}) collective-permute-start(f32[64,128]{1,0:T(8,128)S(1)} %get-tuple-element.256), channel_id=1, source_target_pairs={{0,32},{16,48},{32,0},{48,16},{1,33},{17,49},{33,1},{49,17},{2,34}... | collective-permute-start | bytes 98312 | tf_op jit(solution)/shard_map/ppermute | solution.py:19
  58.2 17.9 %collective-permute-start.11 = (f32[64,128]{1,0:T(8,128)S(1)}, f32[64,128]{1,0:T(8,128)S(1)}, u32[]{:S(2)}, u32[]{:S(2)}) collective-permute-start(f32[64,128]{1,0:T(8,128)S(1)} %get-tuple-element.256), channel_id=1, source_target_pairs={{0,48},{16,0},{32,16},{48,32},{1,49},{17,1},{33,17},{49,33},{2,50}... | collective-permute-start | bytes 98312 | tf_op jit(solution)/shard_map/ppermute | solution.py:19
  78.7 23.0 %collective-permute-start.12 = (f32[64,128]{1,0:T(8,128)S(1)}, f32[64,128]{1,0:T(8,128)S(1)}, u32[]{:S(2)}, u32[]{:S(2)}) collective-permute-start(f32[64,128]{1,0:T(8,128)S(1)} %get-tuple-element.258), channel_id=1, source_target_pairs={{0,16},{16,32},{32,48},{48,0},{1,17},{17,33},{33,49},{49,1},{2,18}... | collective-permute-start | bytes 98312 | tf_op jit(solution)/shard_map/ppermute | solution.py:19
  79.5 22.3 %collective-permute-start.13 = (f32[64,128]{1,0:T(8,128)S(1)}, f32[64,128]{1,0:T(8,128)S(1)}, u32[]{:S(2)}, u32[]{:S(2)}) collective-permute-start(f32[64,128]{1,0:T(8,128)S(1)} %get-tuple-element.258), channel_id=1, source_target_pairs={{0,32},{16,48},{32,0},{48,16},{1,33},{17,49},{33,1},{49,17},{2,34}... | collective-permute-start | bytes 98312 | tf_op jit(solution)/shard_map/ppermute | solution.py:19
  81.6 20.2 %collective-permute-start.14 = (f32[64,128]{1,0:T(8,128)S(1)}, f32[64,128]{1,0:T(8,128)S(1)}, u32[]{:S(2)}, u32[]{:S(2)}) collective-permute-start(f32[64,128]{1,0:T(8,128)S(1)} %get-tuple-element.258), channel_id=1, source_target_pairs={{0,48},{16,0},{32,16},{48,32},{1,49},{17,1},{33,17},{49,33},{2,50}... | collective-permute-start | bytes 98312 | tf_op jit(solution)/shard_map/ppermute | solution.py:19
  104.4 19.5 %collective-permute-start.15 = (f32[64,128]{1,0:T(8,128)S(1)}, f32[64,128]{1,0:T(8,128)S(1)}, u32[]{:S(2)}, u32[]{:S(2)}) collective-permute-start(f32[64,128]{1,0:T(8,128)S(1)} %get-tuple-element.260), channel_id=1, source_target_pairs={{0,16},{16,32},{32,48},{48,0},{1,17},{17,33},{33,49},{49,1},{2,18}... | collective-permute-start | bytes 98312 | tf_op jit(solution)/shard_map/ppermute | solution.py:19
  104.5 19.4 %collective-permute-start.16 = (f32[64,128]{1,0:T(8,128)S(1)}, f32[64,128]{1,0:T(8,128)S(1)}, u32[]{:S(2)}, u32[]{:S(2)}) collective-permute-start(f32[64,128]{1,0:T(8,128)S(1)} %get-tuple-element.260), channel_id=1, source_target_pairs={{0,32},{16,48},{32,0},{48,16},{1,33},{17,49},{33,1},{49,17},{2,34}... | collective-permute-start | bytes 98312 | tf_op jit(solution)/shard_map/ppermute | solution.py:19
  105.9 17.9 %collective-permute-start.17 = (f32[64,128]{1,0:T(8,128)S(1)}, f32[64,128]{1,0:T(8,128)S(1)}, u32[]{:S(2)}, u32[]{:S(2)}) collective-permute-start(f32[64,128]{1,0:T(8,128)S(1)} %get-tuple-element.260), channel_id=1, source_target_pairs={{0,48},{16,0},{32,16},{48,32},{1,49},{17,1},{33,17},{49,33},{2,50}... | collective-permute-start | bytes 98312 | tf_op jit(solution)/shard_map/ppermute | solution.py:19
  126.5 23.0 %collective-permute-start.18 = (f32[64,128]{1,0:T(8,128)S(1)}, f32[64,128]{1,0:T(8,128)S(1)}, u32[]{:S(2)}, u32[]{:S(2)}) collective-permute-start(f32[64,128]{1,0:T(8,128)S(1)} %get-tuple-element.262), channel_id=1, source_target_pairs={{0,16},{16,32},{32,48},{48,0},{1,17},{17,33},{33,49},{49,1},{2,18}... | collective-permute-start | bytes 98312 | tf_op jit(solution)/shard_map/ppermute | solution.py:19
  127.2 22.3 %collective-permute-start.19 = (f32[64,128]{1,0:T(8,128)S(1)}, f32[64,128]{1,0:T(8,128)S(1)}, u32[]{:S(2)}, u32[]{:S(2)}) collective-permute-start(f32[64,128]{1,0:T(8,128)S(1)} %get-tuple-element.262), channel_id=1, source_target_pairs={{0,32},{16,48},{32,0},{48,16},{1,33},{17,49},{33,1},{49,17},{2,34}... | collective-permute-start | bytes 98312 | tf_op jit(solution)/shard_map/ppermute | solution.py:19
  129.4 20.2 %collective-permute-start.20 = (f32[64,128]{1,0:T(8,128)S(1)}, f32[64,128]{1,0:T(8,128)S(1)}, u32[]{:S(2)}, u32[]{:S(2)}) collective-permute-start(f32[64,128]{1,0:T(8,128)S(1)} %get-tuple-element.262), channel_id=1, source_target_pairs={{0,48},{16,0},{32,16},{48,32},{1,49},{17,1},{33,17},{49,33},{2,50}... | collective-permute-start | bytes 98312 | tf_op jit(solution)/shard_map/ppermute | solution.py:19
  152.1 19.7 %collective-permute-start.21 = (f32[64,128]{1,0:T(8,128)S(1)}, f32[64,128]{1,0:T(8,128)S(1)}, u32[]{:S(2)}, u32[]{:S(2)}) collective-permute-start(f32[64,128]{1,0:T(8,128)S(1)} %get-tuple-element.264), channel_id=1, source_target_pairs={{0,16},{16,32},{32,48},{48,0},{1,17},{17,33},{33,49},{49,1},{2,18}... | collective-permute-start | bytes 98312 | tf_op jit(solution)/shard_map/ppermute | solution.py:19
  152.2 19.6 %collective-permute-start.22 = (f32[64,128]{1,0:T(8,128)S(1)}, f32[64,128]{1,0:T(8,128)S(1)}, u32[]{:S(2)}, u32[]{:S(2)}) collective-permute-start(f32[64,128]{1,0:T(8,128)S(1)} %get-tuple-element.264), channel_id=1, source_target_pairs={{0,32},{16,48},{32,0},{48,16},{1,33},{17,49},{33,1},{49,17},{2,34}... | collective-permute-start | bytes 98312 | tf_op jit(solution)/shard_map/ppermute | solution.py:19
  153.7 18.2 %collective-permute-start.23 = (f32[64,128]{1,0:T(8,128)S(1)}, f32[64,128]{1,0:T(8,128)S(1)}, u32[]{:S(2)}, u32[]{:S(2)}) collective-permute-start(f32[64,128]{1,0:T(8,128)S(1)} %get-tuple-element.264), channel_id=1, source_target_pairs={{0,48},{16,0},{32,16},{48,32},{1,49},{17,1},{33,17},{49,33},{2,50}... | collective-permute-start | bytes 98312 | tf_op jit(solution)/shard_map/ppermute | solution.py:19
  174.4 23.0 %collective-permute-start.24 = (f32[64,128]{1,0:T(8,128)S(1)}, f32[64,128]{1,0:T(8,128)S(1)}, u32[]{:S(2)}, u32[]{:S(2)}) collective-permute-start(f32[64,128]{1,0:T(8,128)S(1)} %get-tuple-element.266), channel_id=1, source_target_pairs={{0,16},{16,32},{32,48},{48,0},{1,17},{17,33},{33,49},{49,1},{2,18}... | collective-permute-start | bytes 98312 | tf_op jit(solution)/shard_map/ppermute | solution.py:19
  175.1 22.3 %collective-permute-start.25 = (f32[64,128]{1,0:T(8,128)S(1)}, f32[64,128]{1,0:T(8,128)S(1)}, u32[]{:S(2)}, u32[]{:S(2)}) collective-permute-start(f32[64,128]{1,0:T(8,128)S(1)} %get-tuple-element.266), channel_id=1, source_target_pairs={{0,32},{16,48},{32,0},{48,16},{1,33},{17,49},{33,1},{49,17},{2,34}... | collective-permute-start | bytes 98312 | tf_op jit(solution)/shard_map/ppermute | solution.py:19
  177.3 20.2 %collective-permute-start.26 = (f32[64,128]{1,0:T(8,128)S(1)}, f32[64,128]{1,0:T(8,128)S(1)}, u32[]{:S(2)}, u32[]{:S(2)}) collective-permute-start(f32[64,128]{1,0:T(8,128)S(1)} %get-tuple-element.266), channel_id=1, source_target_pairs={{0,48},{16,0},{32,16},{48,32},{1,49},{17,1},{33,17},{49,33},{2,50}... | collective-permute-start | bytes 98312 | tf_op jit(solution)/shard_map/ppermute | solution.py:19
  200.1 1.8 copy-start.3
  204.2 19.7 %all-to-all-start = ((f32[16,64,128]{2,1,0:T(8,128)}), f32[16,64,128]{2,1,0:T(8,128)S(1)}, u32[]{:S(2)}, u32[]{:S(2)}) async-start(f32[16,64,128]{2,1,0:T(8,128)} %select_reduce_fusion.20), calls=%async_computation | async-start | bytes 1048576 | tf_op jit(solution)/shard_map/while/body/eval_jaxpr/all_to_all | solution.py:41
  208.0 15.8 %collective-permute-start = (f32[64,128]{1,0:T(8,128)S(1)}, f32[64,128]{1,0:T(8,128)S(1)}, u32[]{:S(2)}, u32[]{:S(2)}) collective-permute-start(f32[64,128]{1,0:T(8,128)S(1)} %get-tuple-element.323), channel_id=1, source_target_pairs={{0,48},{16,0},{32,16},{48,32},{1,49},{17,1},{33,17},{49,33},{2,50}... | collective-permute-start | bytes 98312 | tf_op jit(solution)/shard_map/while/body/eval_jaxpr/ppermute | solution.py:19
  208.1 15.8 %collective-permute-start.1 = (f32[64,128]{1,0:T(8,128)S(1)}, f32[64,128]{1,0:T(8,128)S(1)}, u32[]{:S(2)}, u32[]{:S(2)}) collective-permute-start(f32[64,128]{1,0:T(8,128)S(1)} %get-tuple-element.324), channel_id=1, source_target_pairs={{0,32},{16,48},{32,0},{48,16},{1,33},{17,49},{33,1},{49,17},{2,34}... | collective-permute-start | bytes 98312 | tf_op jit(solution)/shard_map/while/body/eval_jaxpr/ppermute | solution.py:19
  209.7 14.2 %collective-permute-start.2 = (f32[64,128]{1,0:T(8,128)S(1)}, f32[64,128]{1,0:T(8,128)S(1)}, u32[]{:S(2)}, u32[]{:S(2)}) collective-permute-start(f32[64,128]{1,0:T(8,128)S(1)} %get-tuple-element.325), channel_id=1, source_target_pairs={{0,16},{16,32},{32,48},{48,0},{1,17},{17,33},{33,49},{49,1},{2,18}... | collective-permute-start | bytes 98312 | tf_op jit(solution)/shard_map/while/body/eval_jaxpr/ppermute | solution.py:19
  227.8 20.4 %all-to-all-start = ((f32[16,64,128]{2,1,0:T(8,128)}), f32[16,64,128]{2,1,0:T(8,128)S(1)}, u32[]{:S(2)}, u32[]{:S(2)}) async-start(f32[16,64,128]{2,1,0:T(8,128)} %select_reduce_fusion.20), calls=%async_computation | async-start | bytes 1048576 | tf_op jit(solution)/shard_map/while/body/eval_jaxpr/all_to_all | solution.py:41
  232.2 16.0 %collective-permute-start = (f32[64,128]{1,0:T(8,128)S(1)}, f32[64,128]{1,0:T(8,128)S(1)}, u32[]{:S(2)}, u32[]{:S(2)}) collective-permute-start(f32[64,128]{1,0:T(8,128)S(1)} %get-tuple-element.323), channel_id=1, source_target_pairs={{0,48},{16,0},{32,16},{48,32},{1,49},{17,1},{33,17},{49,33},{2,50}... | collective-permute-start | bytes 98312 | tf_op jit(solution)/shard_map/while/body/eval_jaxpr/ppermute | solution.py:19
  232.3 16.0 %collective-permute-start.1 = (f32[64,128]{1,0:T(8,128)S(1)}, f32[64,128]{1,0:T(8,128)S(1)}, u32[]{:S(2)}, u32[]{:S(2)}) collective-permute-start(f32[64,128]{1,0:T(8,128)S(1)} %get-tuple-element.324), channel_id=1, source_target_pairs={{0,32},{16,48},{32,0},{48,16},{1,33},{17,49},{33,1},{49,17},{2,34}... | collective-permute-start | bytes 98312 | tf_op jit(solution)/shard_map/while/body/eval_jaxpr/ppermute | solution.py:19
  233.9 14.4 %collective-permute-start.2 = (f32[64,128]{1,0:T(8,128)S(1)}, f32[64,128]{1,0:T(8,128)S(1)}, u32[]{:S(2)}, u32[]{:S(2)}) collective-permute-start(f32[64,128]{1,0:T(8,128)S(1)} %get-tuple-element.325), channel_id=1, source_target_pairs={{0,16},{16,32},{32,48},{48,0},{1,17},{17,33},{33,49},{49,1},{2,18}... | collective-permute-start | bytes 98312 | tf_op jit(solution)/shard_map/while/body/eval_jaxpr/ppermute | solution.py:19
  252.2 20.2 %all-to-all-start = ((f32[16,64,128]{2,1,0:T(8,128)}), f32[16,64,128]{2,1,0:T(8,128)S(1)}, u32[]{:S(2)}, u32[]{:S(2)}) async-start(f32[16,64,128]{2,1,0:T(8,128)} %select_reduce_fusion.20), calls=%async_computation | async-start | bytes 1048576 | tf_op jit(solution)/shard_map/while/body/eval_jaxpr/all_to_all | solution.py:41
  256.4 16.0 %collective-permute-start = (f32[64,128]{1,0:T(8,128)S(1)}, f32[64,128]{1,0:T(8,128)S(1)}, u32[]{:S(2)}, u32[]{:S(2)}) collective-permute-start(f32[64,128]{1,0:T(8,128)S(1)} %get-tuple-element.323), channel_id=1, source_target_pairs={{0,48},{16,0},{32,16},{48,32},{1,49},{17,1},{33,17},{49,33},{2,50}... | collective-permute-start | bytes 98312 | tf_op jit(solution)/shard_map/while/body/eval_jaxpr/ppermute | solution.py:19
  256.5 16.0 %collective-permute-start.1 = (f32[64,128]{1,0:T(8,128)S(1)}, f32[64,128]{1,0:T(8,128)S(1)}, u32[]{:S(2)}, u32[]{:S(2)}) collective-permute-start(f32[64,128]{1,0:T(8,128)S(1)} %get-tuple-element.324), channel_id=1, source_target_pairs={{0,32},{16,48},{32,0},{48,16},{1,33},{17,49},{33,1},{49,17},{2,34}... | collective-permute-start | bytes 98312 | tf_op jit(solution)/shard_map/while/body/eval_jaxpr/ppermute | solution.py:19
  258.0 14.4 %collective-permute-start.2 = (f32[64,128]{1,0:T(8,128)S(1)}, f32[64,128]{1,0:T(8,128)S(1)}, u32[]{:S(2)}, u32[]{:S(2)}) collective-permute-start(f32[64,128]{1,0:T(8,128)S(1)} %get-tuple-element.325), channel_id=1, source_target_pairs={{0,16},{16,32},{32,48},{48,0},{1,17},{17,33},{33,49},{49,1},{2,18}... | collective-permute-start | bytes 98312 | tf_op jit(solution)/shard_map/while/body/eval_jaxpr/ppermute | solution.py:19
  276.4 20.2 %all-to-all-start = ((f32[16,64,128]{2,1,0:T(8,128)}), f32[16,64,128]{2,1,0:T(8,128)S(1)}, u32[]{:S(2)}, u32[]{:S(2)}) async-start(f32[16,64,128]{2,1,0:T(8,128)} %select_reduce_fusion.20), calls=%async_computation | async-start | bytes 1048576 | tf_op jit(solution)/shard_map/while/body/eval_jaxpr/all_to_all | solution.py:41
  280.6 16.0 %collective-permute-start = (f32[64,128]{1,0:T(8,128)S(1)}, f32[64,128]{1,0:T(8,128)S(1)}, u32[]{:S(2)}, u32[]{:S(2)}) collective-permute-start(f32[64,128]{1,0:T(8,128)S(1)} %get-tuple-element.323), channel_id=1, source_target_pairs={{0,48},{16,0},{32,16},{48,32},{1,49},{17,1},{33,17},{49,33},{2,50}... | collective-permute-start | bytes 98312 | tf_op jit(solution)/shard_map/while/body/eval_jaxpr/ppermute | solution.py:19
  280.7 16.0 %collective-permute-start.1 = (f32[64,128]{1,0:T(8,128)S(1)}, f32[64,128]{1,0:T(8,128)S(1)}, u32[]{:S(2)}, u32[]{:S(2)}) collective-permute-start(f32[64,128]{1,0:T(8,128)S(1)} %get-tuple-element.324), channel_id=1, source_target_pairs={{0,32},{16,48},{32,0},{48,16},{1,33},{17,49},{33,1},{49,17},{2,34}... | collective-permute-start | bytes 98312 | tf_op jit(solution)/shard_map/while/body/eval_jaxpr/ppermute | solution.py:19
  282.2 14.4 %collective-permute-start.2 = (f32[64,128]{1,0:T(8,128)S(1)}, f32[64,128]{1,0:T(8,128)S(1)}, u32[]{:S(2)}, u32[]{:S(2)}) collective-permute-start(f32[64,128]{1,0:T(8,128)S(1)} %get-tuple-element.325), channel_id=1, source_target_pairs={{0,16},{16,32},{32,48},{48,0},{1,17},{17,33},{33,49},{49,1},{2,18}... | collective-permute-start | bytes 98312 | tf_op jit(solution)/shard_map/while/body/eval_jaxpr/ppermute | solution.py:19
  300.5 20.2 %all-to-all-start = ((f32[16,64,128]{2,1,0:T(8,128)}), f32[16,64,128]{2,1,0:T(8,128)S(1)}, u32[]{:S(2)}, u32[]{:S(2)}) async-start(f32[16,64,128]{2,1,0:T(8,128)} %select_reduce_fusion.20), calls=%async_computation | async-start | bytes 1048576 | tf_op jit(solution)/shard_map/while/body/eval_jaxpr/all_to_all | solution.py:41
  304.7 16.0 %collective-permute-start = (f32[64,128]{1,0:T(8,128)S(1)}, f32[64,128]{1,0:T(8,128)S(1)}, u32[]{:S(2)}, u32[]{:S(2)}) collective-permute-start(f32[64,128]{1,0:T(8,128)S(1)} %get-tuple-element.323), channel_id=1, source_target_pairs={{0,48},{16,0},{32,16},{48,32},{1,49},{17,1},{33,17},{49,33},{2,50}... | collective-permute-start | bytes 98312 | tf_op jit(solution)/shard_map/while/body/eval_jaxpr/ppermute | solution.py:19
  304.8 16.0 %collective-permute-start.1 = (f32[64,128]{1,0:T(8,128)S(1)}, f32[64,128]{1,0:T(8,128)S(1)}, u32[]{:S(2)}, u32[]{:S(2)}) collective-permute-start(f32[64,128]{1,0:T(8,128)S(1)} %get-tuple-element.324), channel_id=1, source_target_pairs={{0,32},{16,48},{32,0},{48,16},{1,33},{17,49},{33,1},{49,17},{2,34}... | collective-permute-start | bytes 98312 | tf_op jit(solution)/shard_map/while/body/eval_jaxpr/ppermute | solution.py:19
  306.4 14.4 %collective-permute-start.2 = (f32[64,128]{1,0:T(8,128)S(1)}, f32[64,128]{1,0:T(8,128)S(1)}, u32[]{:S(2)}, u32[]{:S(2)}) collective-permute-start(f32[64,128]{1,0:T(8,128)S(1)} %get-tuple-element.325), channel_id=1, source_target_pairs={{0,16},{16,32},{32,48},{48,0},{1,17},{17,33},{33,49},{49,1},{2,18}... | collective-permute-start | bytes 98312 | tf_op jit(solution)/shard_map/while/body/eval_jaxpr/ppermute | solution.py:19
  324.7 20.2 %all-to-all-start = ((f32[16,64,128]{2,1,0:T(8,128)}), f32[16,64,128]{2,1,0:T(8,128)S(1)}, u32[]{:S(2)}, u32[]{:S(2)}) async-start(f32[16,64,128]{2,1,0:T(8,128)} %select_reduce_fusion.20), calls=%async_computation | async-start | bytes 1048576 | tf_op jit(solution)/shard_map/while/body/eval_jaxpr/all_to_all | solution.py:41
  328.9 16.0 %collective-permute-start = (f32[64,128]{1,0:T(8,128)S(1)}, f32[64,128]{1,0:T(8,128)S(1)}, u32[]{:S(2)}, u32[]{:S(2)}) collective-permute-start(f32[64,128]{1,0:T(8,128)S(1)} %get-tuple-element.323), channel_id=1, source_target_pairs={{0,48},{16,0},{32,16},{48,32},{1,49},{17,1},{33,17},{49,33},{2,50}... | collective-permute-start | bytes 98312 | tf_op jit(solution)/shard_map/while/body/eval_jaxpr/ppermute | solution.py:19
  329.0 16.0 %collective-permute-start.1 = (f32[64,128]{1,0:T(8,128)S(1)}, f32[64,128]{1,0:T(8,128)S(1)}, u32[]{:S(2)}, u32[]{:S(2)}) collective-permute-start(f32[64,128]{1,0:T(8,128)S(1)} %get-tuple-element.324), channel_id=1, source_target_pairs={{0,32},{16,48},{32,0},{48,16},{1,33},{17,49},{33,1},{49,17},{2,34}... | collective-permute-start | bytes 98312 | tf_op jit(solution)/shard_map/while/body/eval_jaxpr/ppermute | solution.py:19
  330.5 14.4 %collective-permute-start.2 = (f32[64,128]{1,0:T(8,128)S(1)}, f32[64,128]{1,0:T(8,128)S(1)}, u32[]{:S(2)}, u32[]{:S(2)}) collective-permute-start(f32[64,128]{1,0:T(8,128)S(1)} %get-tuple-element.325), channel_id=1, source_target_pairs={{0,16},{16,32},{32,48},{48,0},{1,17},{17,33},{33,49},{49,1},{2,18}... | collective-permute-start | bytes 98312 | tf_op jit(solution)/shard_map/while/body/eval_jaxpr/ppermute | solution.py:19
  348.9 20.2 %all-to-all-start = ((f32[16,64,128]{2,1,0:T(8,128)}), f32[16,64,128]{2,1,0:T(8,128)S(1)}, u32[]{:S(2)}, u32[]{:S(2)}) async-start(f32[16,64,128]{2,1,0:T(8,128)} %select_reduce_fusion.20), calls=%async_computation | async-start | bytes 1048576 | tf_op jit(solution)/shard_map/while/body/eval_jaxpr/all_to_all | solution.py:41
  353.1 16.0 %collective-permute-start = (f32[64,128]{1,0:T(8,128)S(1)}, f32[64,128]{1,0:T(8,128)S(1)}, u32[]{:S(2)}, u32[]{:S(2)}) collective-permute-start(f32[64,128]{1,0:T(8,128)S(1)} %get-tuple-element.323), channel_id=1, source_target_pairs={{0,48},{16,0},{32,16},{48,32},{1,49},{17,1},{33,17},{49,33},{2,50}... | collective-permute-start | bytes 98312 | tf_op jit(solution)/shard_map/while/body/eval_jaxpr/ppermute | solution.py:19
  353.2 16.0 %collective-permute-start.1 = (f32[64,128]{1,0:T(8,128)S(1)}, f32[64,128]{1,0:T(8,128)S(1)}, u32[]{:S(2)}, u32[]{:S(2)}) collective-permute-start(f32[64,128]{1,0:T(8,128)S(1)} %get-tuple-element.324), channel_id=1, source_target_pairs={{0,32},{16,48},{32,0},{48,16},{1,33},{17,49},{33,1},{49,17},{2,34}... | collective-permute-start | bytes 98312 | tf_op jit(solution)/shard_map/while/body/eval_jaxpr/ppermute | solution.py:19
  354.7 14.4 %collective-permute-start.2 = (f32[64,128]{1,0:T(8,128)S(1)}, f32[64,128]{1,0:T(8,128)S(1)}, u32[]{:S(2)}, u32[]{:S(2)}) collective-permute-start(f32[64,128]{1,0:T(8,128)S(1)} %get-tuple-element.325), channel_id=1, source_target_pairs={{0,16},{16,32},{32,48},{48,0},{1,17},{17,33},{33,49},{49,1},{2,18}... | collective-permute-start | bytes 98312 | tf_op jit(solution)/shard_map/while/body/eval_jaxpr/ppermute | solution.py:19
  372.4 2.0 copy-start.1
where the time goes:
time: 381 us; the launch traced here: 376 us
  blocking collectives  121 us (32%)
  waiting for transfers between devices  106 us (28%)
  starting transfers between devices  82 us (22%)
  matrix products  52.2 us (14%)
  other arithmetic  11.9 us (3%)
    all_gather x7, blocking collectives, gather_sources(): by_col = lax.all_gather(block[None], 'col', axis=0, tiled=True)  121 us
    all_to_all x7, waiting for transfers between devices, push_back(): incoming = lax.all_to_all(slots, 'col', 0, 0, tiled=True).sum(0)  95.6 us
    ppermute x45, starting transfers between devices, shifted(): return lax.ppermute(value, axis, [(i, (i + k) % n) for i in range(n)])  53.8 us
    all_to_all x7, starting transfers between devices, push_back(): incoming = lax.all_to_all(slots, 'col', 0, 0, tiled=True).sum(0)  28.2 us
    dot_general x8, matrix products, apply_transpose(): return jnp.einsum('rs,st->rt', block, inverse, precision=highest)  12.8 us
    ppermute x45, waiting for transfers between devices, shifted(): return lax.ppermute(value, axis, [(i, (i + k) % n) for i in range(n)])  10.4 us
    dot_general x7, matrix products, solve_top(): jnp.einsum('jrs,jts->rt', picked, top_blocks[height - 1], precision=highest)  9.58 us
    dot_general x8, matrix products, apply_inverse(): return jnp.einsum('rs,ts->rt', block, inverse, precision=highest)  8.76 us
  transfers between devices with their start and end apart: 52, of which 10 were waited for; matrix products, arithmetic and copies ran while one was open for 1% of the time, Pallas kernels for 0%

commit v1 on v0

--- a/solution.py
+++ b/solution.py
@@ -58,16 +58,20 @@
     shifts = jnp.arange(n_row, dtype=jnp.int32)
     row_pick = (~is_col)[..., None] & (pull[..., None] == shifts)
     row_push = (~is_col)[..., None] & (push[..., None] == shifts)
-    forward = []
-    for height in range(levels):
-        target = top_right[height] - updates[height]
-        if height > 0:
-            picked = gather_sources(forward[-1], col_pick[height - 1], row_pick[height - 1])
-            target = target - jnp.einsum(
-                "jrs,jts->rt", picked, top_blocks[height - 1], precision=highest
-            )
-        forward.append(apply_inverse(top_inverse[height], target))
-    forward = jnp.stack(forward)
+    first = apply_inverse(top_inverse[0], top_right[0] - updates[0])
+    forward = jnp.zeros_like(updates).at[0].set(first)
+
+    def down(height, carry):
+        latest, forward = carry
+        at = lambda a: lax.dynamic_index_in_dim(a, height, 0, keepdims=False)
+        below = lambda a: lax.dynamic_index_in_dim(a, height - 1, 0, keepdims=False)
+        picked = gather_sources(latest, below(col_pick), below(row_pick))
+        target = at(top_right) - at(updates)
+        target = target - jnp.einsum("jrs,jts->rt", picked, below(top_blocks), precision=highest)
+        latest = apply_inverse(at(top_inverse), target)
+        return latest, lax.dynamic_update_index_in_dim(forward, latest, height, 0)
+
+    forward = lax.fori_loop(1, levels, down, (first, forward))[1]
     current = apply_transpose(top_inverse[levels - 1], forward[levels - 1])
     solved = jnp.zeros_like(forward).at[levels - 1].set(current)
 

time: 381 us -> 384 us (level)
  waiting for transfers between devices: 106 us -> 88.7 us
  starting transfers between devices: 82 us -> 96.8 us
  matrix products: 52.2 us -> 56.4 us
    all_to_all x7, waiting for transfers between devices: 95.6 us -> 78.4 us  [push_back(): incoming = lax.all_to_all(slots, 'col', 0, 0, tiled=True).sum(0)]
    ppermute x45, starting transfers between devices: 53.8 us -> 68.6 us  [shifted(): return lax.ppermute(value, axis, [(i, (i + k) % n) for i in range(n)])]
    dot_general x8, matrix products: 8.76 us -> 13 us  [apply_inverse(): return jnp.einsum('rs,ts->rt', block, inverse, precision=highest)]
where the time goes in v1:
time: 384 us; the launch traced here: 379 us
  blocking collectives  121 us (32%)
  starting transfers between devices  96.8 us (25%)
  waiting for transfers between devices  88.7 us (23%)
  matrix products  56.4 us (15%)
  other arithmetic  12.7 us (3%)
    all_gather x7, blocking collectives, gather_sources(): by_col = lax.all_gather(block[None], 'col', axis=0, tiled=True)  121 us
    all_to_all x7, waiting for transfers between devices, push_back(): incoming = lax.all_to_all(slots, 'col', 0, 0, tiled=True).sum(0)  78.4 us
    ppermute x45, starting transfers between devices, shifted(): return lax.ppermute(value, axis, [(i, (i + k) % n) for i in range(n)])  68.6 us
    all_to_all x7, starting transfers between devices, push_back(): incoming = lax.all_to_all(slots, 'col', 0, 0, tiled=True).sum(0)  28.2 us
    dot_general x8, matrix products, apply_inverse(): return jnp.einsum('rs,ts->rt', block, inverse, precision=highest)  13 us
    dot_general x8, matrix products, apply_transpose(): return jnp.einsum('rs,st->rt', block, inverse, precision=highest)  12.7 us
    ppermute x45, waiting for transfers between devices, shifted(): return lax.ppermute(value, axis, [(i, (i + k) % n) for i in range(n)])  10.4 us
    dot_general x7, matrix products, down(): jnp.einsum('jrs,jts->rt', picked, below(top_blocks), precision=highest)  9.61 us
  transfers between devices with their start and end apart: 52, of which 10 were waited for; matrix products, arithmetic and copies ran while one was open for 1% of the time, Pallas kernels for 0%

profile of v1, /device:TPU:2, one launch (start us, length us, event | category | flops | bytes accessed | tf_op | source)
XLA Modules:
  0.0 379.4 jit_solution(14517170188493728174)
XLA Ops:
  0.6 3.7 fusion.38
  4.3 2.3 fusion.27
  9.3 2.8 collective-permute-start.7
  13.3 4.0 %collective-permute-done.6 = f32[8,64,128]{2,0,1:T(8,128)S(1)} collective-permute-done((f32[8,64,128]{2,0,1:T(8,128)S(1)}, f32[8,64,128]{2,0,1:T(8,128)S(1)}, u32[]{:S(2)}, u32[]{:S(2)}) %collective-permute-start.6) | collective-permute-done | bytes 262176 | tf_op jit(solution)/shard_map/ppermute | solution.py:19
  17.2 2.8 collective-permute-done.7
  20.0 3.5 collective-permute-done.8
  27.8 175.5 %while.40 = (s32[]{:T(128)}, f32[64,128]{1,0:T(8,128)S(1)}, f32[8,64,128]{2,1,0:T(8,128)}, f32[8,64,128]{2,1,0:T(8,128)}, f32[8,64,128]{2,1,0:T(8,128)}, /*index...) while((s32[]{:T(128)}, f32[64,128]{1,0:T(8,128)S(1)}, ...), condition=%wide.region_4.5_spmd, body=%wide.region_1.4_spmd.sunk | while | flops 64307204 | bytes 2917911 | solution.py:74
  27.8 3.1 collective-permute-start
  32.5 21.4 %all-gather.2 = f32[1024,128]{1,0:T(8,128)S(1)} all-gather(f32[64,128]{1,0:T(8,128)S(1)} %get-tuple-element.755), channel_id=2, replica_groups=mesh['leaf'=4,'row'=4,'col'=16] {'col'}, dimensions={0}, use_global_device_ids=true | all-gather | bytes 557056 | tf_op jit(solution)/shard_map/while/body/eval_jaxpr/all_gather | solution.py:32
  55.7 1.7 bitcast_dynamic-update-slice_fusion.4
  57.4 2.3 collective-permute-start
  59.7 1.7 collective-permute-start.1
  61.3 15.7 %all-gather.2 = f32[1024,128]{1,0:T(8,128)S(1)} all-gather(f32[64,128]{1,0:T(8,128)S(1)} %get-tuple-element.755), channel_id=2, replica_groups=mesh['leaf'=4,'row'=4,'col'=16] {'col'}, dimensions={0}, use_global_device_ids=true | all-gather | bytes 557056 | tf_op jit(solution)/shard_map/while/body/eval_jaxpr/all_gather | solution.py:32
  78.8 1.7 bitcast_dynamic-update-slice_fusion.4
  80.5 3.2 collective-permute-start
  84.6 17.4 %all-gather.2 = f32[1024,128]{1,0:T(8,128)S(1)} all-gather(f32[64,128]{1,0:T(8,128)S(1)} %get-tuple-element.755), channel_id=2, replica_groups=mesh['leaf'=4,'row'=4,'col'=16] {'col'}, dimensions={0}, use_global_device_ids=true | all-gather | bytes 557056 | tf_op jit(solution)/shard_map/while/body/eval_jaxpr/all_gather | solution.py:32
  103.8 1.7 bitcast_dynamic-update-slice_fusion.4
  105.5 3.0 collective-permute-start
  108.5 1.7 collective-permute-start.1
  110.2 15.7 %all-gather.2 = f32[1024,128]{1,0:T(8,128)S(1)} all-gather(f32[64,128]{1,0:T(8,128)S(1)} %get-tuple-element.755), channel_id=2, replica_groups=mesh['leaf'=4,'row'=4,'col'=16] {'col'}, dimensions={0}, use_global_device_ids=true | all-gather | bytes 557056 | tf_op jit(solution)/shard_map/while/body/eval_jaxpr/all_gather | solution.py:32
  127.7 1.7 bitcast_dynamic-update-slice_fusion.4
  129.4 3.2 collective-permute-start
  133.5 17.4 %all-gather.2 = f32[1024,128]{1,0:T(8,128)S(1)} all-gather(f32[64,128]{1,0:T(8,128)S(1)} %get-tuple-element.755), channel_id=2, replica_groups=mesh['leaf'=4,'row'=4,'col'=16] {'col'}, dimensions={0}, use_global_device_ids=true | all-gather | bytes 557056 | tf_op jit(solution)/shard_map/while/body/eval_jaxpr/all_gather | solution.py:32
  152.7 1.7 bitcast_dynamic-update-slice_fusion.4
  154.4 3.0 collective-permute-start
  157.4 1.7 collective-permute-start.1
  159.1 15.7 %all-gather.2 = f32[1024,128]{1,0:T(8,128)S(1)} all-gather(f32[64,128]{1,0:T(8,128)S(1)} %get-tuple-element.755), channel_id=2, replica_groups=mesh['leaf'=4,'row'=4,'col'=16] {'col'}, dimensions={0}, use_global_device_ids=true | all-gather | bytes 557056 | tf_op jit(solution)/shard_map/while/body/eval_jaxpr/all_gather | solution.py:32
  176.6 1.7 bitcast_dynamic-update-slice_fusion.4
  178.3 3.2 collective-permute-start
  182.4 17.4 %all-gather.2 = f32[1024,128]{1,0:T(8,128)S(1)} all-gather(f32[64,128]{1,0:T(8,128)S(1)} %get-tuple-element.755), channel_id=2, replica_groups=mesh['leaf'=4,'row'=4,'col'=16] {'col'}, dimensions={0}, use_global_device_ids=true | all-gather | bytes 557056 | tf_op jit(solution)/shard_map/while/body/eval_jaxpr/all_gather | solution.py:32
  201.6 1.7 bitcast_dynamic-update-slice_fusion.4
  205.0 168.9 %while.41 = (s32[]{:T(128)}, f32[64,128]{1,0:T(8,128)S(1)}, f32[8,64,128]{2,1,0:T(8,128)}, f32[8,64,128]{2,1,0:T(8,128)}, pred[7,4,16]{2,1,0:T(4,128)(4,1)S(1)},...) while((s32[]{:T(128)}, f32[64,128]{1,0:T(8,128)S(1)}, ...), condition=%wide.region_9.10_spmd, body=%wide.region_5.9_spmd.sunk | while | flops 64225288 | bytes 4393060 | solution.py:87
  207.3 3.7 all-to-all-start
  211.2 3.1 collective-permute-start.3
  214.3 1.7 collective-permute-start.4
  215.9 11.0 %all-to-all-done = f32[16,64,128]{2,1,0:T(8,128)S(1)} async-done(((f32[16,64,128]{2,1,0:T(8,128)}), f32[16,64,128]{2,1,0:T(8,128)S(1)}, u32[]{:S(2)}, u32[]{:S(2)}) %all-to-all-start) | async-done | bytes 524320 | tf_op jit(solution)/shard_map/while/body/eval_jaxpr/all_to_all | solution.py:41
  227.0 1.7 bitcast_dynamic-update-slice_fusion.5
  230.9 4.2 %all-to-all-start = ((f32[16,64,128]{2,1,0:T(8,128)}), f32[16,64,128]{2,1,0:T(8,128)S(1)}, u32[]{:S(2)}, u32[]{:S(2)}) async-start(f32[16,64,128]{2,1,0:T(8,128)} %select_reduce_fusion.12), calls=%async_computation | async-start | bytes 1048576 | tf_op jit(solution)/shard_map/while/body/eval_jaxpr/all_to_all | solution.py:41
  235.3 3.1 collective-permute-start.3
  238.4 1.7 collective-permute-start.4
  240.1 11.2 %all-to-all-done = f32[16,64,128]{2,1,0:T(8,128)S(1)} async-done(((f32[16,64,128]{2,1,0:T(8,128)}), f32[16,64,128]{2,1,0:T(8,128)S(1)}, u32[]{:S(2)}, u32[]{:S(2)}) %all-to-all-start) | async-done | bytes 524320 | tf_op jit(solution)/shard_map/while/body/eval_jaxpr/all_to_all | solution.py:41
  251.4 1.7 bitcast_dynamic-update-slice_fusion.5
  255.3 4.0 %all-to-all-start = ((f32[16,64,128]{2,1,0:T(8,128)}), f32[16,64,128]{2,1,0:T(8,128)S(1)}, u32[]{:S(2)}, u32[]{:S(2)}) async-start(f32[16,64,128]{2,1,0:T(8,128)} %select_reduce_fusion.12), calls=%async_computation | async-start | bytes 1048576 | tf_op jit(solution)/shard_map/while/body/eval_jaxpr/all_to_all | solution.py:41
  259.5 3.1 collective-permute-start.3
  262.6 1.7 collective-permute-start.4
  264.3 11.2 %all-to-all-done = f32[16,64,128]{2,1,0:T(8,128)S(1)} async-done(((f32[16,64,128]{2,1,0:T(8,128)}), f32[16,64,128]{2,1,0:T(8,128)S(1)}, u32[]{:S(2)}, u32[]{:S(2)}) %all-to-all-start) | async-done | bytes 524320 | tf_op jit(solution)/shard_map/while/body/eval_jaxpr/all_to_all | solution.py:41
  279.5 4.0 %all-to-all-start = ((f32[16,64,128]{2,1,0:T(8,128)}), f32[16,64,128]{2,1,0:T(8,128)S(1)}, u32[]{:S(2)}, u32[]{:S(2)}) async-start(f32[16,64,128]{2,1,0:T(8,128)} %select_reduce_fusion.12), calls=%async_computation | async-start | bytes 1048576 | tf_op jit(solution)/shard_map/while/body/eval_jaxpr/all_to_all | solution.py:41
  283.7 3.1 collective-permute-start.3
  286.8 1.7 collective-permute-start.4
  288.5 11.2 %all-to-all-done = f32[16,64,128]{2,1,0:T(8,128)S(1)} async-done(((f32[16,64,128]{2,1,0:T(8,128)}), f32[16,64,128]{2,1,0:T(8,128)S(1)}, u32[]{:S(2)}, u32[]{:S(2)}) %all-to-all-start) | async-done | bytes 524320 | tf_op jit(solution)/shard_map/while/body/eval_jaxpr/all_to_all | solution.py:41
  303.7 4.0 %all-to-all-start = ((f32[16,64,128]{2,1,0:T(8,128)}), f32[16,64,128]{2,1,0:T(8,128)S(1)}, u32[]{:S(2)}, u32[]{:S(2)}) async-start(f32[16,64,128]{2,1,0:T(8,128)} %select_reduce_fusion.12), calls=%async_computation | async-start | bytes 1048576 | tf_op jit(solution)/shard_map/while/body/eval_jaxpr/all_to_all | solution.py:41
  307.9 3.1 collective-permute-start.3
  310.9 1.7 collective-permute-start.4
  312.6 11.2 %all-to-all-done = f32[16,64,128]{2,1,0:T(8,128)S(1)} async-done(((f32[16,64,128]{2,1,0:T(8,128)}), f32[16,64,128]{2,1,0:T(8,128)S(1)}, u32[]{:S(2)}, u32[]{:S(2)}) %all-to-all-start) | async-done | bytes 524320 | tf_op jit(solution)/shard_map/while/body/eval_jaxpr/all_to_all | solution.py:41
  327.8 4.0 %all-to-all-start = ((f32[16,64,128]{2,1,0:T(8,128)}), f32[16,64,128]{2,1,0:T(8,128)S(1)}, u32[]{:S(2)}, u32[]{:S(2)}) async-start(f32[16,64,128]{2,1,0:T(8,128)} %select_reduce_fusion.12), calls=%async_computation | async-start | bytes 1048576 | tf_op jit(solution)/shard_map/while/body/eval_jaxpr/all_to_all | solution.py:41
  332.0 3.1 collective-permute-start.3
  335.1 1.7 collective-permute-start.4
  336.8 11.2 %all-to-all-done = f32[16,64,128]{2,1,0:T(8,128)S(1)} async-done(((f32[16,64,128]{2,1,0:T(8,128)}), f32[16,64,128]{2,1,0:T(8,128)S(1)}, u32[]{:S(2)}, u32[]{:S(2)}) %all-to-all-start) | async-done | bytes 524320 | tf_op jit(solution)/shard_map/while/body/eval_jaxpr/all_to_all | solution.py:41
  352.0 4.0 %all-to-all-start = ((f32[16,64,128]{2,1,0:T(8,128)}), f32[16,64,128]{2,1,0:T(8,128)S(1)}, u32[]{:S(2)}, u32[]{:S(2)}) async-start(f32[16,64,128]{2,1,0:T(8,128)} %select_reduce_fusion.12), calls=%async_computation | async-start | bytes 1048576 | tf_op jit(solution)/shard_map/while/body/eval_jaxpr/all_to_all | solution.py:41
  356.2 3.1 collective-permute-start.3
  359.3 1.7 collective-permute-start.4
  361.0 11.2 %all-to-all-done = f32[16,64,128]{2,1,0:T(8,128)S(1)} async-done(((f32[16,64,128]{2,1,0:T(8,128)}), f32[16,64,128]{2,1,0:T(8,128)S(1)}, u32[]{:S(2)}, u32[]{:S(2)}) %all-to-all-start) | async-done | bytes 524320 | tf_op jit(solution)/shard_map/while/body/eval_jaxpr/all_to_all | solution.py:41
  375.5 1.9 fusion.32
  377.5 1.9 convolution_bitcast_fusion.2
  (187 shorter events, 52.6 us)
Async XLA Ops:
  0.6 3.7 copy-start
  4.3 2.4 copy-start.3
  4.3 8.3 %copy-start.2 = (s32[7,1,1,4]{0,3,2,1:T(4,128)S(1)}, s32[7,1,1,4]{0,3,2,1:T(4,128)}, u32[]{:S(2)}) copy-start(s32[7,1,1,4]{0,3,2,1:T(4,128)} %param.22) | copy-start | bytes 340
  7.8 9.5 %collective-permute-start.6 = (f32[8,64,128]{2,0,1:T(8,128)S(1)}, f32[8,64,128]{2,0,1:T(8,128)S(1)}, u32[]{:S(2)}, u32[]{:S(2)}) collective-permute-start(f32[8,64,128]{2,0,1:T(8,128)S(1)} %bitcast.207), channel_id=1, source_target_pairs={{0,64},{64,128},{128,192},{192,0},{1,65},{65,129},{129,193},{193,1... | collective-permute-start | bytes 786440 | tf_op jit(solution)/shard_map/ppermute | solution.py:19
  9.3 10.7 %collective-permute-start.7 = (f32[8,64,128]{2,0,1:T(8,128)S(1)}, f32[8,64,128]{2,0,1:T(8,128)S(1)}, u32[]{:S(2)}, u32[]{:S(2)}) collective-permute-start(f32[8,64,128]{2,0,1:T(8,128)S(1)} %bitcast.208), channel_id=1, source_target_pairs={{0,128},{64,192},{128,0},{192,64},{1,129},{65,193},{129,1},{193,65... | collective-permute-start | bytes 786440 | tf_op jit(solution)/shard_map/ppermute | solution.py:19
  12.1 11.4 %collective-permute-start.8 = (f32[8,64,128]{2,0,1:T(8,128)S(1)}, f32[8,64,128]{2,0,1:T(8,128)}, u32[]{:S(2)}, u32[]{:S(2)}) collective-permute-start(f32[8,64,128]{2,0,1:T(8,128)S(1)} %bitcast.209), channel_id=1, source_target_pairs={{0,192},{64,0},{128,64},{192,128},{1,193},{65,1},{129,65},{193,129... | collective-permute-start | bytes 786440 | tf_op jit(solution)/shard_map/ppermute | solution.py:19
  27.8 26.4 %collective-permute-start = (f32[64,128]{1,0:T(8,128)S(1)}, f32[64,128]{1,0:T(8,128)S(1)}, u32[]{:S(2)}, u32[]{:S(2)}) collective-permute-start(f32[64,128]{1,0:T(8,128)S(1)} %get-tuple-element.755), channel_id=1, source_target_pairs={{0,48},{16,0},{32,16},{48,32},{1,49},{17,1},{33,17},{49,33},{2,50}... | collective-permute-start | bytes 98312 | tf_op jit(solution)/shard_map/while/body/eval_jaxpr/ppermute | solution.py:19
  30.9 23.3 %collective-permute-start.1 = (f32[64,128]{1,0:T(8,128)S(1)}, f32[64,128]{1,0:T(8,128)S(1)}, u32[]{:S(2)}, u32[]{:S(2)}) collective-permute-start(f32[64,128]{1,0:T(8,128)S(1)} %get-tuple-element.755), channel_id=1, source_target_pairs={{0,32},{16,48},{32,0},{48,16},{1,33},{17,49},{33,1},{49,17},{2,34}... | collective-permute-start | bytes 98312 | tf_op jit(solution)/shard_map/while/body/eval_jaxpr/ppermute | solution.py:19
  31.5 22.6 %collective-permute-start.2 = (f32[64,128]{1,0:T(8,128)S(1)}, f32[64,128]{1,0:T(8,128)S(1)}, u32[]{:S(2)}, u32[]{:S(2)}) collective-permute-start(f32[64,128]{1,0:T(8,128)S(1)} %get-tuple-element.755), channel_id=1, source_target_pairs={{0,16},{16,32},{32,48},{48,0},{1,17},{17,33},{33,49},{49,1},{2,18}... | collective-permute-start | bytes 98312 | tf_op jit(solution)/shard_map/while/body/eval_jaxpr/ppermute | solution.py:19
  57.4 19.9 %collective-permute-start = (f32[64,128]{1,0:T(8,128)S(1)}, f32[64,128]{1,0:T(8,128)S(1)}, u32[]{:S(2)}, u32[]{:S(2)}) collective-permute-start(f32[64,128]{1,0:T(8,128)S(1)} %get-tuple-element.755), channel_id=1, source_target_pairs={{0,48},{16,0},{32,16},{48,32},{1,49},{17,1},{33,17},{49,33},{2,50}... | collective-permute-start | bytes 98312 | tf_op jit(solution)/shard_map/while/body/eval_jaxpr/ppermute | solution.py:19
  59.7 17.7 %collective-permute-start.1 = (f32[64,128]{1,0:T(8,128)S(1)}, f32[64,128]{1,0:T(8,128)S(1)}, u32[]{:S(2)}, u32[]{:S(2)}) collective-permute-start(f32[64,128]{1,0:T(8,128)S(1)} %get-tuple-element.755), channel_id=1, source_target_pairs={{0,32},{16,48},{32,0},{48,16},{1,33},{17,49},{33,1},{49,17},{2,34}... | collective-permute-start | bytes 98312 | tf_op jit(solution)/shard_map/while/body/eval_jaxpr/ppermute | solution.py:19
  61.3 16.0 %collective-permute-start.2 = (f32[64,128]{1,0:T(8,128)S(1)}, f32[64,128]{1,0:T(8,128)S(1)}, u32[]{:S(2)}, u32[]{:S(2)}) collective-permute-start(f32[64,128]{1,0:T(8,128)S(1)} %get-tuple-element.755), channel_id=1, source_target_pairs={{0,16},{16,32},{32,48},{48,0},{1,17},{17,33},{33,49},{49,1},{2,18}... | collective-permute-start | bytes 98312 | tf_op jit(solution)/shard_map/while/body/eval_jaxpr/ppermute | solution.py:19
  80.5 21.7 %collective-permute-start = (f32[64,128]{1,0:T(8,128)S(1)}, f32[64,128]{1,0:T(8,128)S(1)}, u32[]{:S(2)}, u32[]{:S(2)}) collective-permute-start(f32[64,128]{1,0:T(8,128)S(1)} %get-tuple-element.755), channel_id=1, source_target_pairs={{0,48},{16,0},{32,16},{48,32},{1,49},{17,1},{33,17},{49,33},{2,50}... | collective-permute-start | bytes 98312 | tf_op jit(solution)/shard_map/while/body/eval_jaxpr/ppermute | solution.py:19
  83.8 18.5 %collective-permute-start.1 = (f32[64,128]{1,0:T(8,128)S(1)}, f32[64,128]{1,0:T(8,128)S(1)}, u32[]{:S(2)}, u32[]{:S(2)}) collective-permute-start(f32[64,128]{1,0:T(8,128)S(1)} %get-tuple-element.755), channel_id=1, source_target_pairs={{0,32},{16,48},{32,0},{48,16},{1,33},{17,49},{33,1},{49,17},{2,34}... | collective-permute-start | bytes 98312 | tf_op jit(solution)/shard_map/while/body/eval_jaxpr/ppermute | solution.py:19
  84.4 17.9 %collective-permute-start.2 = (f32[64,128]{1,0:T(8,128)S(1)}, f32[64,128]{1,0:T(8,128)S(1)}, u32[]{:S(2)}, u32[]{:S(2)}) collective-permute-start(f32[64,128]{1,0:T(8,128)S(1)} %get-tuple-element.755), channel_id=1, source_target_pairs={{0,16},{16,32},{32,48},{48,0},{1,17},{17,33},{33,49},{49,1},{2,18}... | collective-permute-start | bytes 98312 | tf_op jit(solution)/shard_map/while/body/eval_jaxpr/ppermute | solution.py:19
  105.5 20.7 %collective-permute-start = (f32[64,128]{1,0:T(8,128)S(1)}, f32[64,128]{1,0:T(8,128)S(1)}, u32[]{:S(2)}, u32[]{:S(2)}) collective-permute-start(f32[64,128]{1,0:T(8,128)S(1)} %get-tuple-element.755), channel_id=1, source_target_pairs={{0,48},{16,0},{32,16},{48,32},{1,49},{17,1},{33,17},{49,33},{2,50}... | collective-permute-start | bytes 98312 | tf_op jit(solution)/shard_map/while/body/eval_jaxpr/ppermute | solution.py:19
  108.5 17.7 %collective-permute-start.1 = (f32[64,128]{1,0:T(8,128)S(1)}, f32[64,128]{1,0:T(8,128)S(1)}, u32[]{:S(2)}, u32[]{:S(2)}) collective-permute-start(f32[64,128]{1,0:T(8,128)S(1)} %get-tuple-element.755), channel_id=1, source_target_pairs={{0,32},{16,48},{32,0},{48,16},{1,33},{17,49},{33,1},{49,17},{2,34}... | collective-permute-start | bytes 98312 | tf_op jit(solution)/shard_map/while/body/eval_jaxpr/ppermute | solution.py:19
  110.2 16.0 %collective-permute-start.2 = (f32[64,128]{1,0:T(8,128)S(1)}, f32[64,128]{1,0:T(8,128)S(1)}, u32[]{:S(2)}, u32[]{:S(2)}) collective-permute-start(f32[64,128]{1,0:T(8,128)S(1)} %get-tuple-element.755), channel_id=1, source_target_pairs={{0,16},{16,32},{32,48},{48,0},{1,17},{17,33},{33,49},{49,1},{2,18}... | collective-permute-start | bytes 98312 | tf_op jit(solution)/shard_map/while/body/eval_jaxpr/ppermute | solution.py:19
  129.4 21.7 %collective-permute-start = (f32[64,128]{1,0:T(8,128)S(1)}, f32[64,128]{1,0:T(8,128)S(1)}, u32[]{:S(2)}, u32[]{:S(2)}) collective-permute-start(f32[64,128]{1,0:T(8,128)S(1)} %get-tuple-element.755), channel_id=1, source_target_pairs={{0,48},{16,0},{32,16},{48,32},{1,49},{17,1},{33,17},{49,33},{2,50}... | collective-permute-start | bytes 98312 | tf_op jit(solution)/shard_map/while/body/eval_jaxpr/ppermute | solution.py:19
  132.7 18.5 %collective-permute-start.1 = (f32[64,128]{1,0:T(8,128)S(1)}, f32[64,128]{1,0:T(8,128)S(1)}, u32[]{:S(2)}, u32[]{:S(2)}) collective-permute-start(f32[64,128]{1,0:T(8,128)S(1)} %get-tuple-element.755), channel_id=1, source_target_pairs={{0,32},{16,48},{32,0},{48,16},{1,33},{17,49},{33,1},{49,17},{2,34}... | collective-permute-start | bytes 98312 | tf_op jit(solution)/shard_map/while/body/eval_jaxpr/ppermute | solution.py:19
  133.3 17.9 %collective-permute-start.2 = (f32[64,128]{1,0:T(8,128)S(1)}, f32[64,128]{1,0:T(8,128)S(1)}, u32[]{:S(2)}, u32[]{:S(2)}) collective-permute-start(f32[64,128]{1,0:T(8,128)S(1)} %get-tuple-element.755), channel_id=1, source_target_pairs={{0,16},{16,32},{32,48},{48,0},{1,17},{17,33},{33,49},{49,1},{2,18}... | collective-permute-start | bytes 98312 | tf_op jit(solution)/shard_map/while/body/eval_jaxpr/ppermute | solution.py:19
  154.4 20.7 %collective-permute-start = (f32[64,128]{1,0:T(8,128)S(1)}, f32[64,128]{1,0:T(8,128)S(1)}, u32[]{:S(2)}, u32[]{:S(2)}) collective-permute-start(f32[64,128]{1,0:T(8,128)S(1)} %get-tuple-element.755), channel_id=1, source_target_pairs={{0,48},{16,0},{32,16},{48,32},{1,49},{17,1},{33,17},{49,33},{2,50}... | collective-permute-start | bytes 98312 | tf_op jit(solution)/shard_map/while/body/eval_jaxpr/ppermute | solution.py:19
  157.4 17.7 %collective-permute-start.1 = (f32[64,128]{1,0:T(8,128)S(1)}, f32[64,128]{1,0:T(8,128)S(1)}, u32[]{:S(2)}, u32[]{:S(2)}) collective-permute-start(f32[64,128]{1,0:T(8,128)S(1)} %get-tuple-element.755), channel_id=1, source_target_pairs={{0,32},{16,48},{32,0},{48,16},{1,33},{17,49},{33,1},{49,17},{2,34}... | collective-permute-start | bytes 98312 | tf_op jit(solution)/shard_map/while/body/eval_jaxpr/ppermute | solution.py:19
  159.1 16.0 %collective-permute-start.2 = (f32[64,128]{1,0:T(8,128)S(1)}, f32[64,128]{1,0:T(8,128)S(1)}, u32[]{:S(2)}, u32[]{:S(2)}) collective-permute-start(f32[64,128]{1,0:T(8,128)S(1)} %get-tuple-element.755), channel_id=1, source_target_pairs={{0,16},{16,32},{32,48},{48,0},{1,17},{17,33},{33,49},{49,1},{2,18}... | collective-permute-start | bytes 98312 | tf_op jit(solution)/shard_map/while/body/eval_jaxpr/ppermute | solution.py:19
  178.3 21.7 %collective-permute-start = (f32[64,128]{1,0:T(8,128)S(1)}, f32[64,128]{1,0:T(8,128)S(1)}, u32[]{:S(2)}, u32[]{:S(2)}) collective-permute-start(f32[64,128]{1,0:T(8,128)S(1)} %get-tuple-element.755), channel_id=1, source_target_pairs={{0,48},{16,0},{32,16},{48,32},{1,49},{17,1},{33,17},{49,33},{2,50}... | collective-permute-start | bytes 98312 | tf_op jit(solution)/shard_map/while/body/eval_jaxpr/ppermute | solution.py:19
  181.5 18.5 %collective-permute-start.1 = (f32[64,128]{1,0:T(8,128)S(1)}, f32[64,128]{1,0:T(8,128)S(1)}, u32[]{:S(2)}, u32[]{:S(2)}) collective-permute-start(f32[64,128]{1,0:T(8,128)S(1)} %get-tuple-element.755), channel_id=1, source_target_pairs={{0,32},{16,48},{32,0},{48,16},{1,33},{17,49},{33,1},{49,17},{2,34}... | collective-permute-start | bytes 98312 | tf_op jit(solution)/shard_map/while/body/eval_jaxpr/ppermute | solution.py:19
  182.2 17.9 %collective-permute-start.2 = (f32[64,128]{1,0:T(8,128)S(1)}, f32[64,128]{1,0:T(8,128)S(1)}, u32[]{:S(2)}, u32[]{:S(2)}) collective-permute-start(f32[64,128]{1,0:T(8,128)S(1)} %get-tuple-element.755), channel_id=1, source_target_pairs={{0,16},{16,32},{32,48},{48,0},{1,17},{17,33},{33,49},{49,1},{2,18}... | collective-permute-start | bytes 98312 | tf_op jit(solution)/shard_map/while/body/eval_jaxpr/ppermute | solution.py:19
  207.3 19.7 %all-to-all-start = ((f32[16,64,128]{2,1,0:T(8,128)}), f32[16,64,128]{2,1,0:T(8,128)S(1)}, u32[]{:S(2)}, u32[]{:S(2)}) async-start(f32[16,64,128]{2,1,0:T(8,128)} %select_reduce_fusion.12), calls=%async_computation | async-start | bytes 1048576 | tf_op jit(solution)/shard_map/while/body/eval_jaxpr/all_to_all | solution.py:41
  211.2 15.8 %collective-permute-start.3 = (f32[64,128]{1,0:T(8,128)S(1)}, f32[64,128]{1,0:T(8,128)S(1)}, u32[]{:S(2)}, u32[]{:S(2)}) collective-permute-start(f32[64,128]{1,0:T(8,128)S(1)} %get-tuple-element.737), channel_id=1, source_target_pairs={{0,48},{16,0},{32,16},{48,32},{1,49},{17,1},{33,17},{49,33},{2,50}... | collective-permute-start | bytes 98312 | tf_op jit(solution)/shard_map/while/body/eval_jaxpr/ppermute | solution.py:19
  214.3 12.8 %collective-permute-start.4 = (f32[64,128]{1,0:T(8,128)S(1)}, f32[64,128]{1,0:T(8,128)S(1)}, u32[]{:S(2)}, u32[]{:S(2)}) collective-permute-start(f32[64,128]{1,0:T(8,128)S(1)} %get-tuple-element.738), channel_id=1, source_target_pairs={{0,32},{16,48},{32,0},{48,16},{1,33},{17,49},{33,1},{49,17},{2,34}... | collective-permute-start | bytes 98312 | tf_op jit(solution)/shard_map/while/body/eval_jaxpr/ppermute | solution.py:19
  215.9 11.1 %collective-permute-start.5 = (f32[64,128]{1,0:T(8,128)S(1)}, f32[64,128]{1,0:T(8,128)S(1)}, u32[]{:S(2)}, u32[]{:S(2)}) collective-permute-start(f32[64,128]{1,0:T(8,128)S(1)} %get-tuple-element.739), channel_id=1, source_target_pairs={{0,16},{16,32},{32,48},{48,0},{1,17},{17,33},{33,49},{49,1},{2,18}... | collective-permute-start | bytes 98312 | tf_op jit(solution)/shard_map/while/body/eval_jaxpr/ppermute | solution.py:19
  230.9 20.4 %all-to-all-start = ((f32[16,64,128]{2,1,0:T(8,128)}), f32[16,64,128]{2,1,0:T(8,128)S(1)}, u32[]{:S(2)}, u32[]{:S(2)}) async-start(f32[16,64,128]{2,1,0:T(8,128)} %select_reduce_fusion.12), calls=%async_computation | async-start | bytes 1048576 | tf_op jit(solution)/shard_map/while/body/eval_jaxpr/all_to_all | solution.py:41
  235.3 16.0 %collective-permute-start.3 = (f32[64,128]{1,0:T(8,128)S(1)}, f32[64,128]{1,0:T(8,128)S(1)}, u32[]{:S(2)}, u32[]{:S(2)}) collective-permute-start(f32[64,128]{1,0:T(8,128)S(1)} %get-tuple-element.737), channel_id=1, source_target_pairs={{0,48},{16,0},{32,16},{48,32},{1,49},{17,1},{33,17},{49,33},{2,50}... | collective-permute-start | bytes 98312 | tf_op jit(solution)/shard_map/while/body/eval_jaxpr/ppermute | solution.py:19
  238.4 13.0 %collective-permute-start.4 = (f32[64,128]{1,0:T(8,128)S(1)}, f32[64,128]{1,0:T(8,128)S(1)}, u32[]{:S(2)}, u32[]{:S(2)}) collective-permute-start(f32[64,128]{1,0:T(8,128)S(1)} %get-tuple-element.738), channel_id=1, source_target_pairs={{0,32},{16,48},{32,0},{48,16},{1,33},{17,49},{33,1},{49,17},{2,34}... | collective-permute-start | bytes 98312 | tf_op jit(solution)/shard_map/while/body/eval_jaxpr/ppermute | solution.py:19
  240.1 11.3 %collective-permute-start.5 = (f32[64,128]{1,0:T(8,128)S(1)}, f32[64,128]{1,0:T(8,128)S(1)}, u32[]{:S(2)}, u32[]{:S(2)}) collective-permute-start(f32[64,128]{1,0:T(8,128)S(1)} %get-tuple-element.739), channel_id=1, source_target_pairs={{0,16},{16,32},{32,48},{48,0},{1,17},{17,33},{33,49},{49,1},{2,18}... | collective-permute-start | bytes 98312 | tf_op jit(solution)/shard_map/while/body/eval_jaxpr/ppermute | solution.py:19
  255.3 20.2 %all-to-all-start = ((f32[16,64,128]{2,1,0:T(8,128)}), f32[16,64,128]{2,1,0:T(8,128)S(1)}, u32[]{:S(2)}, u32[]{:S(2)}) async-start(f32[16,64,128]{2,1,0:T(8,128)} %select_reduce_fusion.12), calls=%async_computation | async-start | bytes 1048576 | tf_op jit(solution)/shard_map/while/body/eval_jaxpr/all_to_all | solution.py:41
  259.5 16.0 %collective-permute-start.3 = (f32[64,128]{1,0:T(8,128)S(1)}, f32[64,128]{1,0:T(8,128)S(1)}, u32[]{:S(2)}, u32[]{:S(2)}) collective-permute-start(f32[64,128]{1,0:T(8,128)S(1)} %get-tuple-element.737), channel_id=1, source_target_pairs={{0,48},{16,0},{32,16},{48,32},{1,49},{17,1},{33,17},{49,33},{2,50}... | collective-permute-start | bytes 98312 | tf_op jit(solution)/shard_map/while/body/eval_jaxpr/ppermute | solution.py:19
  262.6 13.0 %collective-permute-start.4 = (f32[64,128]{1,0:T(8,128)S(1)}, f32[64,128]{1,0:T(8,128)S(1)}, u32[]{:S(2)}, u32[]{:S(2)}) collective-permute-start(f32[64,128]{1,0:T(8,128)S(1)} %get-tuple-element.738), channel_id=1, source_target_pairs={{0,32},{16,48},{32,0},{48,16},{1,33},{17,49},{33,1},{49,17},{2,34}... | collective-permute-start | bytes 98312 | tf_op jit(solution)/shard_map/while/body/eval_jaxpr/ppermute | solution.py:19
  264.3 11.3 %collective-permute-start.5 = (f32[64,128]{1,0:T(8,128)S(1)}, f32[64,128]{1,0:T(8,128)S(1)}, u32[]{:S(2)}, u32[]{:S(2)}) collective-permute-start(f32[64,128]{1,0:T(8,128)S(1)} %get-tuple-element.739), channel_id=1, source_target_pairs={{0,16},{16,32},{32,48},{48,0},{1,17},{17,33},{33,49},{49,1},{2,18}... | collective-permute-start | bytes 98312 | tf_op jit(solution)/shard_map/while/body/eval_jaxpr/ppermute | solution.py:19
  279.5 20.2 %all-to-all-start = ((f32[16,64,128]{2,1,0:T(8,128)}), f32[16,64,128]{2,1,0:T(8,128)S(1)}, u32[]{:S(2)}, u32[]{:S(2)}) async-start(f32[16,64,128]{2,1,0:T(8,128)} %select_reduce_fusion.12), calls=%async_computation | async-start | bytes 1048576 | tf_op jit(solution)/shard_map/while/body/eval_jaxpr/all_to_all | solution.py:41
  283.7 16.0 %collective-permute-start.3 = (f32[64,128]{1,0:T(8,128)S(1)}, f32[64,128]{1,0:T(8,128)S(1)}, u32[]{:S(2)}, u32[]{:S(2)}) collective-permute-start(f32[64,128]{1,0:T(8,128)S(1)} %get-tuple-element.737), channel_id=1, source_target_pairs={{0,48},{16,0},{32,16},{48,32},{1,49},{17,1},{33,17},{49,33},{2,50}... | collective-permute-start | bytes 98312 | tf_op jit(solution)/shard_map/while/body/eval_jaxpr/ppermute | solution.py:19
  286.8 13.0 %collective-permute-start.4 = (f32[64,128]{1,0:T(8,128)S(1)}, f32[64,128]{1,0:T(8,128)S(1)}, u32[]{:S(2)}, u32[]{:S(2)}) collective-permute-start(f32[64,128]{1,0:T(8,128)S(1)} %get-tuple-element.738), channel_id=1, source_target_pairs={{0,32},{16,48},{32,0},{48,16},{1,33},{17,49},{33,1},{49,17},{2,34}... | collective-permute-start | bytes 98312 | tf_op jit(solution)/shard_map/while/body/eval_jaxpr/ppermute | solution.py:19
  288.5 11.3 %collective-permute-start.5 = (f32[64,128]{1,0:T(8,128)S(1)}, f32[64,128]{1,0:T(8,128)S(1)}, u32[]{:S(2)}, u32[]{:S(2)}) collective-permute-start(f32[64,128]{1,0:T(8,128)S(1)} %get-tuple-element.739), channel_id=1, source_target_pairs={{0,16},{16,32},{32,48},{48,0},{1,17},{17,33},{33,49},{49,1},{2,18}... | collective-permute-start | bytes 98312 | tf_op jit(solution)/shard_map/while/body/eval_jaxpr/ppermute | solution.py:19
  303.7 20.2 %all-to-all-start = ((f32[16,64,128]{2,1,0:T(8,128)}), f32[16,64,128]{2,1,0:T(8,128)S(1)}, u32[]{:S(2)}, u32[]{:S(2)}) async-start(f32[16,64,128]{2,1,0:T(8,128)} %select_reduce_fusion.12), calls=%async_computation | async-start | bytes 1048576 | tf_op jit(solution)/shard_map/while/body/eval_jaxpr/all_to_all | solution.py:41
  307.9 16.0 %collective-permute-start.3 = (f32[64,128]{1,0:T(8,128)S(1)}, f32[64,128]{1,0:T(8,128)S(1)}, u32[]{:S(2)}, u32[]{:S(2)}) collective-permute-start(f32[64,128]{1,0:T(8,128)S(1)} %get-tuple-element.737), channel_id=1, source_target_pairs={{0,48},{16,0},{32,16},{48,32},{1,49},{17,1},{33,17},{49,33},{2,50}... | collective-permute-start | bytes 98312 | tf_op jit(solution)/shard_map/while/body/eval_jaxpr/ppermute | solution.py:19
  310.9 13.0 %collective-permute-start.4 = (f32[64,128]{1,0:T(8,128)S(1)}, f32[64,128]{1,0:T(8,128)S(1)}, u32[]{:S(2)}, u32[]{:S(2)}) collective-permute-start(f32[64,128]{1,0:T(8,128)S(1)} %get-tuple-element.738), channel_id=1, source_target_pairs={{0,32},{16,48},{32,0},{48,16},{1,33},{17,49},{33,1},{49,17},{2,34}... | collective-permute-start | bytes 98312 | tf_op jit(solution)/shard_map/while/body/eval_jaxpr/ppermute | solution.py:19
  312.6 11.3 %collective-permute-start.5 = (f32[64,128]{1,0:T(8,128)S(1)}, f32[64,128]{1,0:T(8,128)S(1)}, u32[]{:S(2)}, u32[]{:S(2)}) collective-permute-start(f32[64,128]{1,0:T(8,128)S(1)} %get-tuple-element.739), channel_id=1, source_target_pairs={{0,16},{16,32},{32,48},{48,0},{1,17},{17,33},{33,49},{49,1},{2,18}... | collective-permute-start | bytes 98312 | tf_op jit(solution)/shard_map/while/body/eval_jaxpr/ppermute | solution.py:19
  327.8 20.2 %all-to-all-start = ((f32[16,64,128]{2,1,0:T(8,128)}), f32[16,64,128]{2,1,0:T(8,128)S(1)}, u32[]{:S(2)}, u32[]{:S(2)}) async-start(f32[16,64,128]{2,1,0:T(8,128)} %select_reduce_fusion.12), calls=%async_computation | async-start | bytes 1048576 | tf_op jit(solution)/shard_map/while/body/eval_jaxpr/all_to_all | solution.py:41
  332.0 16.0 %collective-permute-start.3 = (f32[64,128]{1,0:T(8,128)S(1)}, f32[64,128]{1,0:T(8,128)S(1)}, u32[]{:S(2)}, u32[]{:S(2)}) collective-permute-start(f32[64,128]{1,0:T(8,128)S(1)} %get-tuple-element.737), channel_id=1, source_target_pairs={{0,48},{16,0},{32,16},{48,32},{1,49},{17,1},{33,17},{49,33},{2,50}... | collective-permute-start | bytes 98312 | tf_op jit(solution)/shard_map/while/body/eval_jaxpr/ppermute | solution.py:19
  335.1 13.0 %collective-permute-start.4 = (f32[64,128]{1,0:T(8,128)S(1)}, f32[64,128]{1,0:T(8,128)S(1)}, u32[]{:S(2)}, u32[]{:S(2)}) collective-permute-start(f32[64,128]{1,0:T(8,128)S(1)} %get-tuple-element.738), channel_id=1, source_target_pairs={{0,32},{16,48},{32,0},{48,16},{1,33},{17,49},{33,1},{49,17},{2,34}... | collective-permute-start | bytes 98312 | tf_op jit(solution)/shard_map/while/body/eval_jaxpr/ppermute | solution.py:19
  336.8 11.3 %collective-permute-start.5 = (f32[64,128]{1,0:T(8,128)S(1)}, f32[64,128]{1,0:T(8,128)S(1)}, u32[]{:S(2)}, u32[]{:S(2)}) collective-permute-start(f32[64,128]{1,0:T(8,128)S(1)} %get-tuple-element.739), channel_id=1, source_target_pairs={{0,16},{16,32},{32,48},{48,0},{1,17},{17,33},{33,49},{49,1},{2,18}... | collective-permute-start | bytes 98312 | tf_op jit(solution)/shard_map/while/body/eval_jaxpr/ppermute | solution.py:19
  352.0 20.2 %all-to-all-start = ((f32[16,64,128]{2,1,0:T(8,128)}), f32[16,64,128]{2,1,0:T(8,128)S(1)}, u32[]{:S(2)}, u32[]{:S(2)}) async-start(f32[16,64,128]{2,1,0:T(8,128)} %select_reduce_fusion.12), calls=%async_computation | async-start | bytes 1048576 | tf_op jit(solution)/shard_map/while/body/eval_jaxpr/all_to_all | solution.py:41
  356.2 16.0 %collective-permute-start.3 = (f32[64,128]{1,0:T(8,128)S(1)}, f32[64,128]{1,0:T(8,128)S(1)}, u32[]{:S(2)}, u32[]{:S(2)}) collective-permute-start(f32[64,128]{1,0:T(8,128)S(1)} %get-tuple-element.737), channel_id=1, source_target_pairs={{0,48},{16,0},{32,16},{48,32},{1,49},{17,1},{33,17},{49,33},{2,50}... | collective-permute-start | bytes 98312 | tf_op jit(solution)/shard_map/while/body/eval_jaxpr/ppermute | solution.py:19
  359.3 13.0 %collective-permute-start.4 = (f32[64,128]{1,0:T(8,128)S(1)}, f32[64,128]{1,0:T(8,128)S(1)}, u32[]{:S(2)}, u32[]{:S(2)}) collective-permute-start(f32[64,128]{1,0:T(8,128)S(1)} %get-tuple-element.738), channel_id=1, source_target_pairs={{0,32},{16,48},{32,0},{48,16},{1,33},{17,49},{33,1},{49,17},{2,34}... | collective-permute-start | bytes 98312 | tf_op jit(solution)/shard_map/while/body/eval_jaxpr/ppermute | solution.py:19
  361.0 11.3 %collective-permute-start.5 = (f32[64,128]{1,0:T(8,128)S(1)}, f32[64,128]{1,0:T(8,128)S(1)}, u32[]{:S(2)}, u32[]{:S(2)}) collective-permute-start(f32[64,128]{1,0:T(8,128)S(1)} %get-tuple-element.739), channel_id=1, source_target_pairs={{0,16},{16,32},{32,48},{48,0},{1,17},{17,33},{33,49},{49,1},{2,18}... | collective-permute-start | bytes 98312 | tf_op jit(solution)/shard_map/while/body/eval_jaxpr/ppermute | solution.py:19
  375.5 2.0 copy-start.1
